TPU v7x, 128 devices: a whole 4x4x4 slice. The times are simulated.
128 devices in a mesh: prow: 8 (over x, core), pcol: 16 (over y, z).
Axes of the slice: x: 4, y: 4, z: 4, core: 2. Of those that a mesh axis runs over, the one named last changes fastest.
Arguments:
- basis: bfloat16 [512, 256], replicated, may hold values from -0.25 to 0.25
- potentials: float32 [8, 512], replicated, may hold values from -6 to 6
- orbitals: bfloat16 [64, 512], P('pcol'), may hold values from -6 to 6
- chan_orbital: int32 [256], replicated, may hold values from 0 to 63
- pair_list: int32 [24576, 3], P(('prow', 'pcol')), may hold values from 0 to 255, as said below
- slot_list: int32 [24576], P(('prow', 'pcol')), may hold values from 0 to 255
- coefs: float32 [24576, 2], P(('prow', 'pcol')), may hold values from -6 to 6
- exchange_ops: bfloat16 [24576, 128, 256], P(('prow', 'pcol')), may hold values from -1.1953125 to 1.1953125
Outputs:
- hamiltonian: bfloat16 [32, 8, 2, 16, 256, 256], P(None, 'prow', None, 'pcol')
Inputs may be any that keep to these rules, and one draw needn't show every extreme that they name: `pair_list`: columns 0 and 1 are channels a, b; column 2 is a multipole order below 8. (b // 16 - a // 16) modulo 256 // 16 is below 2. Terms of one device with the same slot s have the same two channels, and the block (a, b) belongs to owner s // 2 in prow-major order: a % 8 and b % 16 are that owner's prow and pcol indices.
All inputs are finite; a program needn't handle non-finite values.
Results may differ from a plain program's by a relative error of at most 0.0058.
Values may be sent and summed in bfloat16 or wider, within the bound.
No kernel may reach another device: no remote copies, remote signals or barrier semaphores. Data moves between devices by JAX's collectives and lax.ppermute only.
A program may use at most 320 MiB of HBM per device.

v0:
```python
import jax
import jax.numpy as jnp
from jax import lax
from jax.sharding import PartitionSpec as P

CAP = 2
BAND = 2
RBLK = 32


def build_tiles(weights_group, exchange_group, basis):
    weights_group = lax.optimization_barrier(weights_group)
    scaled = (
        weights_group.astype(jnp.float32)[:, :, None] * basis.astype(jnp.float32)[None]
    ).astype(jnp.bfloat16)
    inner_rows = basis[: exchange_group.shape[1]]
    local_part = jnp.einsum("qa,gqb->gab", basis, scaled, preferred_element_type=jnp.float32)
    exchange_part = jnp.einsum(
        "qa,gqb->gab", inner_rows, exchange_group, preferred_element_type=jnp.float32
    )
    return (local_part + exchange_part).astype(jnp.bfloat16)


def sum_blocks(built_tiles, idents, block_count):
    select = (jnp.arange(block_count, dtype=jnp.int32)[:, None] == idents[None, :]).astype(
        jnp.bfloat16
    )
    spline_width = built_tiles.shape[1]
    summed = jnp.dot(
        select,
        built_tiles.reshape(built_tiles.shape[0], spline_width * spline_width),
        preferred_element_type=jnp.float32,
    )
    return summed.reshape(block_count, spline_width, spline_width)


def on_device(basis, potentials, orbitals, chan_orbital, pair_list, slot_list, coefs, exchange_ops):
    all_orbitals = lax.all_gather(orbitals, "pcol", axis=0, tiled=True)
    row_devs = lax.axis_size("prow")
    col_devs = lax.axis_size("pcol")
    slot_count = row_devs * col_devs * CAP
    chan_count = chan_orbital.shape[0]
    orb_count = all_orbitals.shape[0]
    point_count = basis.shape[0]
    spline_count = basis.shape[1]
    inner_count = exchange_ops.shape[1]
    term_count = exchange_ops.shape[0]
    col_groups = chan_count // col_devs
    block_count = RBLK * BAND
    first_chan = pair_list[:, 0]
    second_chan = pair_list[:, 1]
    multipole = pair_list[:, 2]
    channels = jnp.arange(chan_count, dtype=jnp.int32)
    orb_ids = jnp.arange(orb_count, dtype=jnp.int32)
    first_orb = jnp.sum(
        jnp.where(first_chan[:, None] == channels[None, :], chan_orbital[None, :], 0), axis=1
    )
    second_orb = jnp.sum(
        jnp.where(second_chan[:, None] == channels[None, :], chan_orbital[None, :], 0), axis=1
    )
    first_rows = jnp.dot(
        (first_orb[:, None] == orb_ids[None, :]).astype(jnp.bfloat16),
        all_orbitals,
        preferred_element_type=jnp.float32,
    )
    second_rows = jnp.dot(
        (second_orb[:, None] == orb_ids[None, :]).astype(jnp.bfloat16),
        all_orbitals,
        preferred_element_type=jnp.float32,
    )
    pick_pot = (
        multipole[:, None] == jnp.arange(potentials.shape[0], dtype=jnp.int32)[None, :]
    ).astype(jnp.float32)
    pot_rows = jnp.dot(pick_pot, potentials, precision=lax.Precision.HIGHEST)
    radial = coefs[:, 0:1] * pot_rows + coefs[:, 1:2] * (first_rows * second_rows)
    matches = slot_list[None, :] == jnp.arange(slot_count, dtype=jnp.int32)[:, None]
    slot_weight = jnp.dot(
        matches.astype(jnp.float32), radial, precision=lax.Precision.HIGHEST
    ).astype(jnp.bfloat16)
    exchange_rows = exchange_ops.reshape(term_count, inner_count * spline_count)
    slot_exchange = jnp.dot(
        matches.astype(jnp.bfloat16), exchange_rows, preferred_element_type=jnp.float32
    ).astype(jnp.bfloat16)
    slot_exchange = slot_exchange.reshape(slot_count, inner_count, spline_count)
    offset = jnp.mod(second_chan // col_devs - first_chan // col_devs, col_groups)
    block_index = first_chan // row_devs * BAND + offset
    slot_ids = jnp.max(jnp.where(matches, block_index[None, :], -1), axis=1)
    built_tiles = lax.map(
        lambda slot_group: build_tiles(slot_group[0], slot_group[1], basis),
        (
            slot_weight.reshape(slot_count // 16, 16, point_count),
            slot_exchange.reshape(slot_count // 16, 16, inner_count, spline_count),
        ),
    )
    built_tiles = built_tiles.reshape(row_devs, col_devs, CAP, spline_count, spline_count)
    received, idents = (
        lax.all_to_all(
            lax.all_to_all(built_tiles, "prow", split_axis=0, concat_axis=0, tiled=True),
            "pcol",
            split_axis=1,
            concat_axis=1,
            tiled=True,
        ),
        lax.all_to_all(
            lax.all_to_all(
                slot_ids.reshape(row_devs, col_devs, CAP),
                "prow",
                split_axis=0,
                concat_axis=0,
                tiled=True,
            ),
            "pcol",
            split_axis=1,
            concat_axis=1,
            tiled=True,
        ),
    )
    blocks = sum_blocks(
        received.reshape(slot_count, spline_count, spline_count),
        idents.reshape(slot_count),
        block_count,
    )
    return blocks.astype(jnp.bfloat16).reshape(RBLK, 1, BAND, 1, spline_count, spline_count)


def solution(mesh):
    placed = (
        P(),
        P(),
        P("pcol", None),
        P(),
        P(("prow", "pcol"), None),
        P(("prow", "pcol")),
        P(("prow", "pcol"), None),
        P(("prow", "pcol"), None, None),
    )
    return jax.shard_map(
        on_device,
        mesh=mesh,
        in_specs=placed,
        out_specs=P(None, "prow", None, "pcol", None, None),
        check_vma=False,
    )
```

profile of v0, /device:TPU:80, one launch (start us, length us, event | category | flops | bytes accessed | tf_op | source)
XLA Modules:
  0.0 1376.1 jit_solution(16522838021894493454)
XLA Ops:
  2.5 4.3 all-to-all-start
  8.5 21.0 %all-gather = bf16[16,4,512]{2,1,0:T(4,128)(2,1)S(1)} all-gather(bf16[1,4,512]{2,1,0:T(4,128)(2,1)} %bitcast.71), channel_id=1, replica_groups=mesh['prow'=8,'pcol'=16] {'pcol'}, dimensions={0}, use_global_device_ids=true | all-gather | bytes 69632 | tf_op jit(solution)/shard_map/all_gather | solution.py:38
  31.6 13.9 %copy.50 = bf16[24,8,128,256]{3,1,2,0:T(8,128)(2,1)} copy(bf16[24,8,128,256]{3,2,1,0:T(8,128)(2,1)} %bitcast.62) | data formatting | bytes 25165824
  45.5 12.7 convolution_convert_fusion
  58.2 15.7 %copy.51 = bf16[32,8,128,256]{3,2,1,0:T(8,128)(2,1)} copy(bf16[32,8,128,256]{3,1,2,0:T(8,128)(2,1)} %bitcast.58) | data formatting | bytes 33554432
  73.9 144.8 %while.10 = (s32[]{:T(128)}, bf16[16,16,256,256]{3,2,1,0:T(8,128)(2,1)}, bf16[16,16,512]{2,1,0:T(8,128)(2,1)S(1)}, bf16[512,256]{1,0:T(8,128)(2,1)S(1)}, bf16[16,16,128,256]{3,2,1,0:T(8,128)(2,1)}, /*index=5*/s32[]{:T(128)}) while((s32[]{:T(128)}, bf16[16,16,256,256]{3,2,1,0:T(8,128)(2,1)}, bf16[16,16,512]{2,1,0:T(8,128)(2,1)S(1)}, ...), condition=%wide.region_4.5_spmd, body=%wide.region_3.4_spmd.sunk | while | flops 1348476928 | bytes 21676120 | solution.py:88
  75.3 3.3 fusion.40
  78.6 2.8 copy.56
  84.4 3.3 fusion.40
  87.7 2.8 copy.56
  93.4 3.3 fusion.40
  96.7 2.8 copy.56
  102.5 3.3 fusion.40
  105.8 2.8 copy.56
  111.5 3.3 fusion.40
  114.8 2.8 copy.56
  120.6 3.3 fusion.40
  123.9 2.8 copy.56
  129.7 3.3 fusion.40
  133.0 2.8 copy.56
  138.7 3.3 fusion.40
  142.0 2.8 copy.56
  147.7 3.3 fusion.40
  151.0 2.8 copy.56
  156.8 3.3 fusion.40
  160.1 2.8 copy.56
  165.8 3.3 fusion.40
  169.1 2.8 copy.56
  174.9 3.3 fusion.40
  178.2 2.8 copy.56
  184.0 3.3 fusion.40
  187.3 2.8 copy.56
  193.0 3.3 fusion.40
  196.3 2.8 copy.56
  202.1 3.3 fusion.40
  205.4 2.8 copy.56
  211.1 3.3 fusion.40
  218.7 7.2 all-to-all-start.2
  226.6 363.6 %all-to-all-done.2 = bf16[8,16,2,256,256]{4,3,2,1,0:T(8,128)(2,1)} async-done(((bf16[8,16,2,256,256]{4,3,2,1,0:T(8,128)(2,1)}), bf16[8,16,2,256,256]{4,3,2,1,0:T(8,128)(2,1)}, u32[]{:S(2)}, u32[]{:S(2)}) %all-to-all-start.2) | async-done | bytes 33554464 | tf_op jit(solution)/shard_map/all_to_all | solution.py:98
  590.2 8.3 all-to-all-start.1
  598.5 23.0 %copy.42 = bf16[8,16,2,256,256]{4,3,2,0,1:T(8,128)(2,1)} copy(bf16[8,16,2,256,256]{4,3,2,1,0:T(8,128)(2,1)} %all-to-all-done.2) | data formatting | bytes 67108864 | tf_op jit(solution)/shard_map/all_to_all | solution.py:98
  621.4 7.2 all-to-all-start.3
  629.0 618.7 %all-to-all-done.3 = bf16[8,16,2,256,256]{4,3,2,0,1:T(8,128)(2,1)} async-done(((bf16[8,16,2,256,256]{4,3,2,0,1:T(8,128)(2,1)}), bf16[8,16,2,256,256]{4,3,2,0,1:T(8,128)(2,1)}, u32[]{:S(2)}, u32[]{:S(2)}) %all-to-all-start.3) | async-done | bytes 33554464 | tf_op jit(solution)/shard_map/all_to_all | solution.py:97
  1247.7 23.0 %copy.43 = bf16[8,16,2,256,256]{4,3,2,1,0:T(8,128)(2,1)} copy(bf16[8,16,2,256,256]{4,3,2,0,1:T(8,128)(2,1)} %all-to-all-done.3) | data formatting | bytes 67108864 | tf_op jit(solution)/shard_map/all_to_all | solution.py:97
  1270.7 31.0 %copy.52 = bf16[32,8,256,256]{3,1,2,0:T(8,128)(2,1)} copy(bf16[32,8,256,256]{3,2,1,0:T(8,128)(2,1)} %bitcast.56) | data formatting | bytes 67108864
  1301.7 44.0 %copy.44 = bf16[65536,256]{1,0:T(8,128)(2,1)} copy(bf16[65536,256]{0,1:T(8,128)(2,1)} %bitcast.57) | data formatting | bytes 67108864 | tf_op jit(solution)/shard_map/dot_general | solution.py:29
  1345.6 18.9 %convolution_convert_fusion.1 = bf16[64,256,256]{2,0,1:T(8,128)(2,1)} fusion(bf16[256,256,256]{2,1,0:T(8,128)(2,1)} %bitcast.55, s32[256]{0:T(256)S(1)} %eq.101), kind=kOutput, calls=%fused_computation.15 | convolution fusion | flops 2151694336 | bytes 41944064 | tf_op jit(solution)/shard_map/dot_general | solution.py:29
  1364.5 11.5 copy.46
  (107 shorter events, 56.1 us)
Async XLA Ops:
  0.0 30.0 %copy-start = (f32[8,512]{1,0:T(8,128)S(1)}, f32[8,512]{1,0:T(8,128)}, u32[]{:S(2)}) copy-start(f32[8,512]{1,0:T(8,128)} %param.11) | copy-start | bytes 49156
  0.0 45.5 %copy-start.3 = (s32[192]{0:T(256)S(1)}, s32[192]{0:T(256)}, u32[]{:S(2)}) copy-start(s32[192]{0:T(256)} %param.15) | copy-start | bytes 2308
  2.5 216.2 %all-to-all-start = ((s32[8,16,2]{1,2,0:T(2,128)}), s32[8,16,2]{1,2,0:T(2,128)S(1)}, u32[]{:S(2)}, u32[]{:S(2)}) async-start(s32[8,16,2]{1,2,0:T(2,128)} %copy.37), calls=%async_computation | async-start | bytes 16384 | tf_op jit(solution)/shard_map/all_to_all | solution.py:105
  58.2 15.7 %copy-start.2 = (bf16[512,256]{1,0:T(8,128)(2,1)S(1)}, bf16[512,256]{1,0:T(8,128)(2,1)}, u32[]{:S(2)}) copy-start(bf16[512,256]{1,0:T(8,128)(2,1)} %param.10) | copy-start | bytes 786436
  218.7 371.5 %all-to-all-start.2 = ((bf16[8,16,2,256,256]{4,3,2,1,0:T(8,128)(2,1)}), bf16[8,16,2,256,256]{4,3,2,1,0:T(8,128)(2,1)}, u32[]{:S(2)}, u32[]{:S(2)}) async-start(bf16[8,16,2,256,256]{4,3,2,1,0:T(8,128)(2,1)} %bitcast.60), calls=%async_computation.2 | async-start | bytes 67108864 | tf_op jit(solution)/shard_map/all_to_all | solution.py:98
  590.2 31.2 %all-to-all-start.1 = ((s32[8,16,2]{0,2,1:T(2,128)}), s32[8,16,2]{0,2,1:T(2,128)S(1)}, u32[]{:S(2)}, u32[]{:S(2)}) async-start(s32[8,16,2]{0,2,1:T(2,128)} %copy.38), calls=%async_computation.1 | async-start | bytes 32768 | tf_op jit(solution)/shard_map/all_to_all | solution.py:104
  621.4 626.3 %all-to-all-start.3 = ((bf16[8,16,2,256,256]{4,3,2,0,1:T(8,128)(2,1)}), bf16[8,16,2,256,256]{4,3,2,0,1:T(8,128)(2,1)}, u32[]{:S(2)}, u32[]{:S(2)}) async-start(bf16[8,16,2,256,256]{4,3,2,0,1:T(8,128)(2,1)} %copy.42), calls=%async_computation.3 | async-start | bytes 67108864 | tf_op jit(solution)/shard_map/all_to_all | solution.py:97
  1345.6 30.5 %copy-start.1 = (f32[8,512]{1,0:T(8,128)S(1)}, f32[8,512]{1,0:T(8,128)}, u32[]{:S(2)}) copy-start(f32[8,512]{1,0:T(8,128)} %param.11) | copy-start | bytes 49156
where the time goes:
time: 1380 us
  waiting for transfers between devices  982 us (71%)
  local copies, waits for them, and re-layouts  237 us (17%)
  matrix products  107 us (8%)
  starting transfers between devices  27 us (2%)
  blocking collectives  21 us (2%)
    all_to_all x1, waiting for transfers between devices, on_device(): lax.all_to_all(lax.all_to_all(built_tiles, 'prow', split_axis=0, concat_a...  619 us
    all_to_all x1, waiting for transfers between devices, on_device(): lax.all_to_all(built_tiles, 'prow', split_axis=0, concat_axis=0, tiled=True)  364 us
    dynamic_update_slice x32, local copies, waits for them, and re-layouts, on_device(): lax.map(lambda slot_group: build_tiles(slot_group[0], slot_group[1], basi...  69.1 us
    unnamed x12, local copies, waits for them, and re-layouts  60.6 us
    dot_general x16, matrix products, build_tiles(): jnp.einsum('qa,gqb->gab', inner_rows, exchange_group, preferred_element_t...  52.9 us
    dot_general x1, local copies, waits for them, and re-layouts, sum_blocks(): jnp.dot(select, built_tiles.reshape(built_tiles.shape[0], spline_width *...  44 us
  transfers between devices with their start and end apart: 4, of which 2 were waited for; matrix products, arithmetic and copies ran while one was open for 16% of the time, Pallas kernels for 0%

commit v1 on v0

v1 whole, which is shorter than its diff:
```python
import jax
import jax.numpy as jnp
from jax import lax
from jax.sharding import PartitionSpec as P

CAP = 2
BAND = 2
RBLK = 32


def split_bf16(values):
    high = values.astype(jnp.bfloat16)
    low = (values - high.astype(jnp.float32)).astype(jnp.bfloat16)
    return high, low


def on_device(basis, potentials, orbitals, chan_orbital, pair_list, slot_list, coefs, exchange_ops):
    all_orbitals = lax.all_gather(orbitals, "pcol", axis=0, tiled=True)
    row_devs = lax.axis_size("prow")
    col_devs = lax.axis_size("pcol")
    slot_count = row_devs * col_devs * CAP
    chan_count = chan_orbital.shape[0]
    orb_count = all_orbitals.shape[0]
    point_count = basis.shape[0]
    spline_count = basis.shape[1]
    inner_count = exchange_ops.shape[1]
    term_count = exchange_ops.shape[0]
    col_groups = chan_count // col_devs
    block_count = RBLK * BAND
    first_chan = pair_list[:, 0]
    second_chan = pair_list[:, 1]
    multipole = pair_list[:, 2]
    channels = jnp.arange(chan_count, dtype=jnp.int32)
    orb_ids = jnp.arange(orb_count, dtype=jnp.int32)
    first_orb = jnp.sum(
        jnp.where(first_chan[:, None] == channels[None, :], chan_orbital[None, :], 0), axis=1
    )
    second_orb = jnp.sum(
        jnp.where(second_chan[:, None] == channels[None, :], chan_orbital[None, :], 0), axis=1
    )
    first_rows = jnp.dot(
        (first_orb[:, None] == orb_ids[None, :]).astype(jnp.bfloat16),
        all_orbitals,
        preferred_element_type=jnp.float32,
    )
    second_rows = jnp.dot(
        (second_orb[:, None] == orb_ids[None, :]).astype(jnp.bfloat16),
        all_orbitals,
        preferred_element_type=jnp.float32,
    )
    pick_pot = (
        multipole[:, None] == jnp.arange(potentials.shape[0], dtype=jnp.int32)[None, :]
    ).astype(jnp.float32)
    pot_rows = jnp.dot(pick_pot, potentials, precision=lax.Precision.HIGHEST)
    radial = coefs[:, 0:1] * pot_rows + coefs[:, 1:2] * (first_rows * second_rows)
    matches = slot_list[None, :] == jnp.arange(slot_count, dtype=jnp.int32)[:, None]
    slot_weight = jnp.dot(
        matches.astype(jnp.float32), radial, precision=lax.Precision.HIGHEST
    ).astype(jnp.bfloat16)
    exchange_rows = exchange_ops.reshape(term_count, inner_count * spline_count)
    slot_exchange = jnp.dot(
        matches.astype(jnp.bfloat16), exchange_rows, preferred_element_type=jnp.float32
    ).astype(jnp.bfloat16)
    offset = jnp.mod(second_chan // col_devs - first_chan // col_devs, col_groups)
    block_index = first_chan // row_devs * BAND + offset
    slot_ids = jnp.max(jnp.where(matches, block_index[None, :], -1), axis=1)

    payload = inner_count * spline_count + point_count + 1
    width = -(-payload // 128) * 128
    packed = jnp.concatenate(
        [
            slot_exchange,
            slot_weight,
            slot_ids.astype(jnp.bfloat16)[:, None],
            jnp.zeros((slot_count, width - payload), jnp.bfloat16),
        ],
        axis=1,
    )
    received = lax.all_to_all(packed, ("prow", "pcol"), 0, 0, tiled=True)

    idents = received[:, payload - 1].astype(jnp.float32).astype(jnp.int32)
    select = (jnp.arange(block_count, dtype=jnp.int32)[:, None] == idents[None, :]).astype(
        jnp.bfloat16
    )
    summed = jnp.dot(select, received[:, : payload - 1], preferred_element_type=jnp.float32)
    exchange_sum = summed[:, : inner_count * spline_count].reshape(
        block_count, inner_count, spline_count
    )
    weight_sum = summed[:, inner_count * spline_count :]
    basis_float = basis.astype(jnp.float32)
    scaled_high, scaled_low = split_bf16(weight_sum[:, :, None] * basis_float[None])
    exchange_high, exchange_low = split_bf16(exchange_sum)
    inner_rows = basis[:inner_count]
    tiles = (
        jnp.einsum("qa,gqb->gab", basis, scaled_high, preferred_element_type=jnp.float32)
        + jnp.einsum("qa,gqb->gab", basis, scaled_low, preferred_element_type=jnp.float32)
        + jnp.einsum("qa,gqb->gab", inner_rows, exchange_high, preferred_element_type=jnp.float32)
        + jnp.einsum("qa,gqb->gab", inner_rows, exchange_low, preferred_element_type=jnp.float32)
    )
    return tiles.astype(jnp.bfloat16).reshape(RBLK, 1, BAND, 1, spline_count, spline_count)


def solution(mesh):
    placed = (
        P(),
        P(),
        P("pcol", None),
        P(),
        P(("prow", "pcol"), None),
        P(("prow", "pcol")),
        P(("prow", "pcol"), None),
        P(("prow", "pcol"), None, None),
    )
    return jax.shard_map(
        on_device,
        mesh=mesh,
        in_specs=placed,
        out_specs=P(None, "prow", None, "pcol", None, None),
        check_vma=False,
    )
```

time: 1380 us -> 492 us (0.36)
  the two profiles are of different devices: /device:TPU:80 before, /device:TPU:23 now
where the time goes in v1:
time: 492 us; the launch traced here: 490 us
  waiting for transfers between devices  240 us (49%)
  local copies, waits for them, and re-layouts  139 us (28%)
  matrix products  74.7 us (15%)
  blocking collectives  18.1 us (4%)
  starting transfers between devices  14.7 us (3%)
    all_to_all x1, waiting for transfers between devices, on_device(): received = lax.all_to_all(packed, ('prow', 'pcol'), 0, 0, tiled=True)  240 us
    concatenate x3, local copies, waits for them, and re-layouts, on_device(): jnp.concatenate([slot_exchange, slot_weight, slot_ids.astype(jnp.bfloat16...  49.1 us
    unnamed x16, local copies, waits for them, and re-layouts  38.1 us
    all_to_all x1, local copies, waits for them, and re-layouts, on_device(): received = lax.all_to_all(packed, ('prow', 'pcol'), 0, 0, tiled=True)  25.3 us
    dot_general x1, matrix products, on_device(): jnp.einsum('qa,gqb->gab', inner_rows, exchange_low, preferred_element_typ...  24.9 us
    all_gather x1, blocking collectives, on_device(): all_orbitals = lax.all_gather(orbitals, 'pcol', axis=0, tiled=True)  18.1 us
    all_to_all x1, starting transfers between devices, on_device(): received = lax.all_to_all(packed, ('prow', 'pcol'), 0, 0, tiled=True)  14.7 us
    dot_general x1, matrix products, on_device(): jnp.dot(matches.astype(jnp.bfloat16), exchange_rows, preferred_element_ty...  12.7 us
  transfers between devices with their start and end apart: 1, of which 1 were waited for; matrix products, arithmetic and copies ran while one was open for 0% of the time, Pallas kernels for 0%

profile of v1, /device:TPU:23, one launch (start us, length us, event | category | flops | bytes accessed | tf_op | source)
XLA Modules:
  0.0 489.6 jit_solution(6347302952289938058)
XLA Ops:
  0.0 0.0 copy-start
  0.0 0.0 copy-start.4
  0.0 0.8 fusion.31
  0.8 0.8 fusion.30
  1.6 0.8 select_reduce_fusion
  2.4 0.9 select_reduce_fusion.1
  3.3 0.2 convert_element_type.87
  3.6 18.1 %all-gather = bf16[16,4,512]{2,1,0:T(4,128)(2,1)S(1)} all-gather(bf16[1,4,512]{2,1,0:T(4,128)(2,1)} %bitcast.40), channel_id=1, replica_groups=mesh['prow'=8,'pcol'=16] {'pcol'}, dimensions={0}, use_global_device_ids=true | all-gather | bytes 69632 | tf_op jit(solution)/shard_map/all_gather | solution.py:18
  21.7 0.2 fusion.19
  22.0 0.3 fusion.14
  22.3 0.0 copy-done
  22.3 0.4 fusion.13
  22.6 1.2 convolution_convert_fusion.1
  23.8 0.1 concatenate.9
  23.9 13.9 %copy.34 = bf16[24,8,128,256]{3,1,2,0:T(8,128)(2,1)} copy(bf16[24,8,128,256]{3,2,1,0:T(8,128)(2,1)} %bitcast.32) | data formatting | bytes 25165824
  37.8 0.0 copy-done.4
  37.8 12.7 %convolution_convert_fusion = bf16[256,32768]{1,0:T(8,128)(2,1)} fusion(bf16[192,32768]{1,0:T(8,128)(2,1)} %bitcast.28, s32[192]{0:T(256)S(1)} %copy-done.4), kind=kOutput, calls=%fused_computation.2 | convolution fusion | flops 3229663232 | bytes 29360896 | tf_op jit(solution)/shard_map/dot_general | solution.py:61
  50.6 27.1 %concatenate.8 = bf16[128,2,32768]{2,1,0:T(2,128)(2,1)} reshape(bf16[256,32768]{1,0:T(8,128)(2,1)} %convolution_convert_fusion) | data formatting | bytes 33554432 | tf_op jit(solution)/shard_map/concatenate | solution.py:70
  77.6 14.1 %constant_dynamic-update-slice_fusion.1 = bf16[128,2,33408]{2,1,0:T(2,128)(2,1)} fusion(bf16[128,2,32768]{2,1,0:T(2,128)(2,1)} %concatenate.8), kind=kLoop, calls=%fused_computation.47 | loop fusion | bytes 33554432
  91.8 0.9 constant_dynamic-update-slice_fusion
  92.7 3.3 dynamic-update-slice.2
  96.0 21.9 %dynamic-update-slice.3 = bf16[128,2,33408]{2,1,0:T(2,128)(2,1)} dynamic-update-slice(bf16[128,2,33408]{2,1,0:T(2,128)(2,1)} %dynamic-update-slice.2, bf16[128,2,127]{2,1,0:T(2,128)(2,1)S(1)} %broadcast_in_dim.52, s32[]{} %constant.60, s32[]{} %constant.60, s32[]{} %constant.63) | dynamic-update-slice | bytes 130052 | tf_op jit(solution)/shard_map/concatenate | solution.py:70
  117.9 0.0 copy-start.3
  117.9 14.7 %all-to-all-start = ((bf16[128,2,33408]{2,1,0:T(2,128)(2,1)}), bf16[128,2,33408]{2,1,0:T(2,128)(2,1)}, u32[]{:S(2)}, u32[]{:S(2)}) async-start(bf16[128,2,33408]{2,1,0:T(2,128)(2,1)} %dynamic-update-slice.3), calls=%async_computation | async-start | bytes 34209792 | tf_op jit(solution)/shard_map/all_to_all | solution.py:79
  132.6 0.0 copy-done.3
  132.6 0.1 copy.30
  132.8 239.9 %all-to-all-done = bf16[128,2,33408]{2,1,0:T(2,128)(2,1)} async-done(((bf16[128,2,33408]{2,1,0:T(2,128)(2,1)}), bf16[128,2,33408]{2,1,0:T(2,128)(2,1)}, u32[]{:S(2)}, u32[]{:S(2)}) %all-to-all-start) | async-done | bytes 17104928 | tf_op jit(solution)/shard_map/all_to_all | solution.py:79
  372.7 25.3 %all_to_all.7 = bf16[256,33408]{1,0:T(8,128)(2,1)} reshape(bf16[128,2,33408]{2,1,0:T(2,128)(2,1)} %all-to-all-done) | data formatting | bytes 34209792 | tf_op jit(solution)/shard_map/all_to_all | solution.py:79
  398.1 1.0 convert_reduce_fusion
  399.0 7.5 %fusion.2 = f32[64,33280]{1,0:T(8,128)S(1)} fusion(bf16[256,33408]{1,0:T(8,128)(2,1)} %all_to_all.7, s32[256]{0:T(256)S(1)} %convert_reduce_fusion), kind=kOutput, calls=%fused_computation.5 | convolution fusion | flops 1090535424 | bytes 25560064 | tf_op jit(solution)/shard_map/dot_general | solution.py:85
  406.5 3.9 slice.43
  410.5 8.0 %fusion.4 = f32[64,256,256]{2,1,0:T(8,128)} fusion(f32[512,256]{0,1:T(8,128)S(1)} %copy.30, f32[64,512]{1,0:T(8,128)S(1)} %slice.42, bf16[512,256]{1,0:T(8,128)(2,1)S(1)} %copy-done.3), kind=kOutput, calls=%fused_computation.7 | convolution fusion | flops 4336910336 | bytes 17694720 | tf_op jit(solution)/shard_map/qa,gqb->gab/dot_general | solution.py:96
  418.5 0.0 copy-start.2
  418.5 8.0 %fusion.1 = f32[64,256,256]{2,1,0:T(8,128)} fusion(f32[512,256]{0,1:T(8,128)S(1)} %copy.30, f32[64,512]{1,0:T(8,128)S(1)} %slice.42, bf16[512,256]{1,0:T(8,128)(2,1)S(1)} %copy-done.3), kind=kOutput, calls=%fused_computation.4 | convolution fusion | flops 4311744512 | bytes 17694720 | tf_op jit(solution)/shard_map/qa,gqb->gab/dot_general | solution.py:95
  426.5 0.0 copy-done.2
  426.5 5.9 %copy.35 = f32[8,8,128,256]{3,2,1,0:T(8,128)} copy(f32[8,8,128,256]{3,1,2,0:T(8,128)S(1)} %bitcast.30) | data formatting | bytes 16777216
  432.4 9.0 %copy.31 = f32[64,128,256]{1,2,0:T(8,128)} copy(f32[64,128,256]{2,1,0:T(8,128)} %bitcast.31) | data formatting | bytes 16777216 | tf_op jit(solution)/shard_map/reshape | solution.py:86
  441.4 11.4 %fusion.11 = f32[64,256,256]{2,1,0:T(8,128)} fusion(f32[64,128,256]{1,2,0:T(8,128)} %copy.31, bf16[512,256]{1,0:T(8,128)(2,1)S(1)} %copy-done.3), kind=kOutput, calls=%fused_computation.15 | convolution fusion | flops 1075838976 | bytes 25231360 | tf_op jit(solution)/shard_map/qa,gqb->gab/dot_general | solution.py:97
  452.8 0.0 copy-start.1
  452.8 24.9 %add_convert_fusion = bf16[64,256,256]{2,1,0:T(8,128)(2,1)} fusion(f32[64,256,256]{2,1,0:T(8,128)} %fusion.11, f32[64,256,256]{2,1,0:T(8,128)} %fusion.1, f32[64,256,256]{2,1,0:T(8,128)} %fusion.4, f32[64,128,256]{1,2,0:T(8,128)} %copy.31, bf16[512,256]{1,0:T(8,128)(2,1)S(1)} %copy-done.3), kind=kOutput, calls=%fused_computation.8 | convolution fusion | flops 1098907648 | bytes 67174400 | tf_op jit(solution)/shard_map/qa,gqb->gab/dot_general | solution.py:98
  477.7 11.9 %copy.33 = bf16[32,1,2,1,256,256]{5,4,3,2,1,0:T(8,128)(2,1)} copy(bf16[32,1,2,1,256,256]{4,5,2,0,3,1:T(8,128)(2,1)} %bitcast.29) | data formatting | bytes 16777216 | tf_op jit(solution)/shard_map/reshape | solution.py:100
  489.6 0.0 copy-done.1
  (5 shorter events, 0.1 us)
Async XLA Ops:
  0.0 22.3 %copy-start = (f32[8,512]{1,0:T(8,128)S(1)}, f32[8,512]{1,0:T(8,128)}, u32[]{:S(2)}) copy-start(f32[8,512]{1,0:T(8,128)} %param.9) | copy-start | bytes 49156
  0.0 37.8 %copy-start.4 = (s32[192]{0:T(256)S(1)}, s32[192]{0:T(256)}, u32[]{:S(2)}) copy-start(s32[192]{0:T(256)} %param.13) | copy-start | bytes 2308
  117.9 14.8 %copy-start.3 = (bf16[512,256]{1,0:T(8,128)(2,1)S(1)}, bf16[512,256]{1,0:T(8,128)(2,1)}, u32[]{:S(2)}) copy-start(bf16[512,256]{1,0:T(8,128)(2,1)} %param.8) | copy-start | bytes 786436
  117.9 254.8 %all-to-all-start = ((bf16[128,2,33408]{2,1,0:T(2,128)(2,1)}), bf16[128,2,33408]{2,1,0:T(2,128)(2,1)}, u32[]{:S(2)}, u32[]{:S(2)}) async-start(bf16[128,2,33408]{2,1,0:T(2,128)(2,1)} %dynamic-update-slice.3), calls=%async_computation | async-start | bytes 34209792 | tf_op jit(solution)/shard_map/all_to_all | solution.py:79
  418.5 8.0 %copy-start.2 = (f32[64,32768]{1,0:T(8,128)S(1)}, f32[64,32768]{1,0:T(8,128)}, u32[]{:S(2)}) copy-start(f32[64,32768]{1,0:T(8,128)} %slice.43) | copy-start | bytes 25165828
  452.8 36.8 %copy-start.1 = (f32[8,512]{1,0:T(8,128)S(1)}, f32[8,512]{1,0:T(8,128)}, u32[]{:S(2)}) copy-start(f32[8,512]{1,0:T(8,128)} %param.9) | copy-start | bytes 49156

commit v2 on v1

v2 whole, which is shorter than its diff:
```python
import jax
import jax.numpy as jnp
from jax import lax
from jax.experimental import pallas as pl
from jax.sharding import PartitionSpec as P

CAP = 2
BAND = 2
RBLK = 32


def split_bf16(values):
    high = values.astype(jnp.bfloat16)
    low = (values - high.astype(jnp.float32)).astype(jnp.bfloat16)
    return high, low


def tile_kernel(weight_ref, exchange_ref, basis_t_ref, basis_ref, inner_t_ref, out_ref):
    left = basis_t_ref[...].astype(jnp.float32) * weight_ref[0]
    left_high, left_low = split_bf16(left)
    basis = basis_ref[...]
    acc = jnp.dot(left_high, basis, preferred_element_type=jnp.float32)
    acc += jnp.dot(left_low, basis, preferred_element_type=jnp.float32)
    exchange_high, exchange_low = split_bf16(exchange_ref[0])
    inner_t = inner_t_ref[...]
    acc += jnp.dot(inner_t, exchange_high, preferred_element_type=jnp.float32)
    acc += jnp.dot(inner_t, exchange_low, preferred_element_type=jnp.float32)
    out_ref[0] = acc.astype(out_ref.dtype)


def build_blocks(weight_sum, exchange_sum, basis):
    block_count, point_count = weight_sum.shape
    inner_count, spline_count = exchange_sum.shape[1:]
    basis_t = basis.T
    inner_t = basis[:inner_count].T
    return pl.pallas_call(
        tile_kernel,
        grid=(block_count,),
        in_specs=[
            pl.BlockSpec((1, 1, point_count), lambda g: (g, 0, 0)),
            pl.BlockSpec((1, inner_count, spline_count), lambda g: (g, 0, 0)),
            pl.BlockSpec((spline_count, point_count), lambda g: (0, 0)),
            pl.BlockSpec((point_count, spline_count), lambda g: (0, 0)),
            pl.BlockSpec((spline_count, inner_count), lambda g: (0, 0)),
        ],
        out_specs=pl.BlockSpec((1, spline_count, spline_count), lambda g: (g, 0, 0)),
        out_shape=jax.ShapeDtypeStruct((block_count, spline_count, spline_count), jnp.bfloat16),
    )(weight_sum.reshape(block_count, 1, point_count), exchange_sum, basis_t, basis, inner_t)


def on_device(basis, potentials, orbitals, chan_orbital, pair_list, slot_list, coefs, exchange_ops):
    row_devs = lax.axis_size("prow")
    col_devs = lax.axis_size("pcol")
    slot_count = row_devs * col_devs * CAP
    chan_count = chan_orbital.shape[0]
    point_count = basis.shape[0]
    spline_count = basis.shape[1]
    inner_count = exchange_ops.shape[1]
    col_groups = chan_count // col_devs
    block_count = RBLK * BAND
    first_chan = pair_list[:, 0]
    second_chan = pair_list[:, 1]
    multipole = pair_list[:, 2]
    matches = slot_list[None, :] == jnp.arange(slot_count, dtype=jnp.int32)[:, None]

    slot_exchange = jnp.einsum(
        "st,tqb->sqb",
        matches.astype(jnp.bfloat16),
        exchange_ops,
        preferred_element_type=jnp.float32,
    ).astype(jnp.bfloat16)
    received_exchange = lax.all_to_all(slot_exchange, ("prow", "pcol"), 0, 0, tiled=True)

    all_orbitals = lax.all_gather(orbitals, "pcol", axis=0, tiled=True)
    orb_count = all_orbitals.shape[0]
    channels = jnp.arange(chan_count, dtype=jnp.int32)
    orb_ids = jnp.arange(orb_count, dtype=jnp.int32)
    first_orb = jnp.sum(
        jnp.where(first_chan[:, None] == channels[None, :], chan_orbital[None, :], 0), axis=1
    )
    second_orb = jnp.sum(
        jnp.where(second_chan[:, None] == channels[None, :], chan_orbital[None, :], 0), axis=1
    )
    first_rows = jnp.dot(
        (first_orb[:, None] == orb_ids[None, :]).astype(jnp.bfloat16),
        all_orbitals,
        preferred_element_type=jnp.float32,
    )
    second_rows = jnp.dot(
        (second_orb[:, None] == orb_ids[None, :]).astype(jnp.bfloat16),
        all_orbitals,
        preferred_element_type=jnp.float32,
    )
    pick_pot = (
        multipole[:, None] == jnp.arange(potentials.shape[0], dtype=jnp.int32)[None, :]
    ).astype(jnp.float32)
    pot_rows = jnp.dot(pick_pot, potentials, precision=lax.Precision.HIGHEST)
    radial = coefs[:, 0:1] * pot_rows + coefs[:, 1:2] * (first_rows * second_rows)
    slot_weight = jnp.dot(
        matches.astype(jnp.float32), radial, precision=lax.Precision.HIGHEST
    ).astype(jnp.bfloat16)
    offset = jnp.mod(second_chan // col_devs - first_chan // col_devs, col_groups)
    block_index = first_chan // row_devs * BAND + offset
    slot_ids = jnp.max(jnp.where(matches, block_index[None, :], -1), axis=1)

    width = -(-(point_count + 1) // 128) * 128
    small = jnp.concatenate(
        [
            slot_weight,
            slot_ids.astype(jnp.bfloat16)[:, None],
            jnp.zeros((slot_count, width - point_count - 1), jnp.bfloat16),
        ],
        axis=1,
    )
    received_small = lax.all_to_all(small, ("prow", "pcol"), 0, 0, tiled=True)

    idents = received_small[:, point_count].astype(jnp.float32).astype(jnp.int32)
    select = (jnp.arange(block_count, dtype=jnp.int32)[:, None] == idents[None, :]).astype(
        jnp.bfloat16
    )
    weight_sum = jnp.dot(
        select, received_small[:, :point_count], preferred_element_type=jnp.float32
    )
    exchange_sum = jnp.einsum(
        "gs,sqb->gqb", select, received_exchange, preferred_element_type=jnp.float32
    )
    blocks = build_blocks(weight_sum, exchange_sum, basis)
    return blocks.reshape(RBLK, 1, BAND, 1, spline_count, spline_count)


def solution(mesh):
    placed = (
        P(),
        P(),
        P("pcol", None),
        P(),
        P(("prow", "pcol"), None),
        P(("prow", "pcol")),
        P(("prow", "pcol"), None),
        P(("prow", "pcol"), None, None),
    )
    return jax.shard_map(
        on_device,
        mesh=mesh,
        in_specs=placed,
        out_specs=P(None, "prow", None, "pcol", None, None),
        check_vma=False,
    )
```

time: 492 us -> 395 us (0.80)
  local copies, waits for them, and re-layouts: 139 us -> 29.7 us
  Pallas kernels: 0 us -> 45.1 us
  matrix products: 74.7 us -> 37.6 us
  waiting for transfers between devices: 240 us -> 230 us
  starting transfers between devices: 14.7 us -> 24.5 us
    concatenate x3 -> x2, local copies, waits for them, and re-layouts: 49.1 us -> 0.18 us  [on_device(): jnp.concatenate([slot_weight, slot_ids.astype(jnp.bfloat16)[:, None], jnp...]
    pallas_call x0 -> x1, Pallas kernels: none -> 45.1 us  [build_blocks(): pl.pallas_call(tile_kernel, grid=(block_count,), in_specs=[pl.BlockSpec((...]
    unnamed x16 -> x10, local copies, waits for them, and re-layouts: 38.1 us -> 0.18 us
    dot_general x6 -> x3, matrix products: 72.7 us -> 35.6 us  [the longest x1 17.8 us: on_device(): jnp.einsum('st,tqb->sqb', matches.astype(jnp.bfloat16), exchange_ops, pre...]
    all_to_all x1, local copies, waits for them, and re-layouts: 25.3 us -> 0.12 us  [on_device(): received_small = lax.all_to_all(small, ('prow', 'pcol'), 0, 0, tiled=True)]
    reshape x2 -> x1, local copies, waits for them, and re-layouts: 20.8 us -> 0.74 us  [build_blocks(): weight_sum.reshape(block_count, 1, point_count)]
    convert_element_type x1, local copies, waits for them, and re-layouts: 0.14 us -> 17.9 us  [on_device(): slot_exchange = jnp.einsum('st,tqb->sqb', matches.astype(jnp.bfloat16), e...]
    all_to_all x1 -> x2, waiting for transfers between devices: 240 us -> 230 us  [the longest x1 230 us: on_device(): lax.all_to_all(slot_exchange, ('prow', 'pcol'), 0, 0, tiled=True)]
  transfers between devices with their start and end apart: 1 -> 2, of which waited for: 1 -> 1; matrix products, arithmetic and copies ran while one was open for 0% -> 10% of each run, Pallas kernels for 0% -> 0%
where the time goes in v2:
time: 395 us; the launch traced here: 388 us
  waiting for transfers between devices  230 us (58%)
  Pallas kernels  45.1 us (11%)
  matrix products  37.6 us (10%)
  local copies, waits for them, and re-layouts  29.7 us (8%)
  starting transfers between devices  24.5 us (6%)
  blocking collectives  18.1 us (5%)
    all_to_all x1, waiting for transfers between devices, on_device(): lax.all_to_all(slot_exchange, ('prow', 'pcol'), 0, 0, tiled=True)  230 us
    pallas_call x1, Pallas kernels, build_blocks(): pl.pallas_call(tile_kernel, grid=(block_count,), in_specs=[pl.BlockSpec((...  45.1 us
    all_gather x1, blocking collectives, on_device(): all_orbitals = lax.all_gather(orbitals, 'pcol', axis=0, tiled=True)  18.1 us
    convert_element_type x1, local copies, waits for them, and re-layouts, on_device(): slot_exchange = jnp.einsum('st,tqb->sqb', matches.astype(jnp.bfloat16), e...  17.9 us
    dot_general x1, matrix products, on_device(): jnp.einsum('st,tqb->sqb', matches.astype(jnp.bfloat16), exchange_ops, pre...  17.8 us
    dot_general x1, matrix products, on_device(): jnp.einsum('gs,sqb->gqb', select, received_exchange, preferred_element_ty...  17.6 us
    all_to_all x1, starting transfers between devices, on_device(): received_small = lax.all_to_all(small, ('prow', 'pcol'), 0, 0, tiled=True)  14.3 us
    all_to_all x1, starting transfers between devices, on_device(): lax.all_to_all(slot_exchange, ('prow', 'pcol'), 0, 0, tiled=True)  10.2 us
  transfers between devices with their start and end apart: 2, of which 1 were waited for; matrix products, arithmetic and copies ran while one was open for 10% of the time, Pallas kernels for 0%

profile of v2, /device:TPU:23, one launch (start us, length us, event | category | flops | bytes accessed | tf_op | source)
XLA Modules:
  0.0 388.1 jit_solution(14941486761368870323)
XLA Ops:
  0.0 0.0 copy-start
  0.0 0.8 fusion.25
  0.8 0.9 select_reduce_fusion.1
  1.8 18.1 %all-gather = bf16[16,4,512]{2,1,0:T(4,128)(2,1)S(1)} all-gather(bf16[1,4,512]{2,1,0:T(4,128)(2,1)} %bitcast.30), channel_id=1, replica_groups=mesh['prow'=8,'pcol'=16] {'pcol'}, dimensions={0}, use_global_device_ids=true | all-gather | bytes 69632 | tf_op jit(solution)/shard_map/all_gather | solution.py:74
  19.9 0.8 fusion.26
  20.7 0.2 fusion.15
  20.9 0.3 fusion.8
  21.2 0.0 copy-done
  21.2 0.4 fusion.7
  21.6 1.2 convolution_convert_fusion
  22.7 0.1 concatenate.6
  22.9 0.8 select_reduce_fusion
  23.7 0.2 convert_element_type.51
  23.9 0.1 pad.2.clone
  24.0 1.1 maximum_maximum_fusion
  25.1 14.3 %all-to-all-start = ((bf16[128,2,640]{2,1,0:T(2,128)(2,1)}), bf16[128,2,640]{2,1,0:T(2,128)(2,1)S(1)}, u32[]{:S(2)}, u32[]{:S(2)}) async-start(bf16[128,2,640]{2,1,0:T(2,128)(2,1)} %maximum_maximum_fusion), calls=%async_computation | async-start | bytes 655360 | tf_op jit(solution)/shard_map/all_to_all | solution.py:115
  39.4 17.8 %fusion.4 = bf16[256,128,256]{2,0,1:T(8,128)(2,1)} fusion(bf16[192,128,256]{2,1,0:T(8,128)(2,1)} %param.15, s32[192]{0:T(256)} %param.13), kind=kOutput, calls=%fused_computation.4 | convolution fusion | flops 3229663232 | bytes 29360896 | tf_op jit(solution)/shard_map/st,tqb->sqb/dot_general | solution.py:66
  57.2 17.9 %copy.35 = bf16[256,128,256]{2,1,0:T(8,128)(2,1)} copy(bf16[256,128,256]{2,0,1:T(8,128)(2,1)} %fusion.4) | data formatting | bytes 33554432 | tf_op jit(solution)/shard_map/convert_element_type | solution.py:71
  75.2 0.0 copy-start.3
  75.2 0.0 all-to-all-done
  75.2 10.2 %all-to-all-start.1 = ((bf16[256,128,256]{2,1,0:T(8,128)(2,1)}), bf16[256,128,256]{2,1,0:T(8,128)(2,1)}, u32[]{:S(2)}, u32[]{:S(2)}) async-start(bf16[256,128,256]{2,1,0:T(8,128)(2,1)} %copy.35), calls=%async_computation.1 | async-start | bytes 33554432 | tf_op jit(solution)/shard_map/all_to_all | solution.py:72
  85.4 0.0 copy-done.3
  85.5 0.1 copy.37
  85.6 0.0 copy-start.2
  85.6 0.7 slice_bitcast_fusion.inner_t_ref
  86.3 0.1 all_to_all.10
  86.4 0.1 convert_reduce_fusion
  86.5 0.2 fusion.9
  86.7 0.7 reshape.115.weight_ref
  87.5 230.0 %all-to-all-done.1 = bf16[256,128,256]{2,1,0:T(8,128)(2,1)} async-done(((bf16[256,128,256]{2,1,0:T(8,128)(2,1)}), bf16[256,128,256]{2,1,0:T(8,128)(2,1)}, u32[]{:S(2)}, u32[]{:S(2)}) %all-to-all-start.1) | async-done | bytes 16777248 | tf_op jit(solution)/shard_map/all_to_all | solution.py:72
  317.4 0.0 copy-start.1
  317.4 17.6 %fusion = f32[64,128,256]{2,0,1:T(8,128)S(1)} fusion(bf16[256,128,256]{2,1,0:T(8,128)(2,1)} %all-to-all-done.1, s32[256]{0:T(256)S(1)} %convert_reduce_fusion), kind=kOutput, calls=%fused_computation | convolution fusion | flops 1073758208 | bytes 25166848 | tf_op jit(solution)/shard_map/gs,sqb->gqb/dot_general | solution.py:124
  335.0 8.1 %copy.39.exchange_ref = f32[64,128,256]{2,1,0:T(8,128)} copy(f32[64,128,256]{2,0,1:T(8,128)S(1)} %fusion) | data formatting | bytes 16777216 | tf_op jit(solution)/shard_map/gs,sqb->gqb/dot_general | solution.py:124
  343.1 0.0 copy-done.2
  343.1 45.1 %shard_map.82 = bf16[64,256,256]{2,1,0:T(8,128)(2,1)} custom-call(f32[64,1,512]{2,1,0:T(1,128)} %reshape.115.weight_ref, f32[64,128,256]{2,1,0:T(8,128)} %copy.39.exchange_ref, bf16[256,512]{1,0:T(8,128)(2,1)} %bitcast.22, bf16[512,256]{1,0:T(8,128)(2,1)} %basis_ref.1, bf16[256,128]{1,0:T(8,128)(2,1)} %slice_bitcast_fusion.inner_t_ref), custom_call_target="tpu_custom_call" | custom-call | tf_op jit(solution)/shard_map/pallas_call | solution.py:36
  388.1 0.0 copy-done.1
  (4 shorter events, 0.1 us)
Async XLA Ops:
  0.0 21.2 %copy-start = (f32[8,512]{1,0:T(8,128)S(1)}, f32[8,512]{1,0:T(8,128)}, u32[]{:S(2)}) copy-start(f32[8,512]{1,0:T(8,128)} %param.9) | copy-start | bytes 49156
  25.1 50.1 %all-to-all-start = ((bf16[128,2,640]{2,1,0:T(2,128)(2,1)}), bf16[128,2,640]{2,1,0:T(2,128)(2,1)S(1)}, u32[]{:S(2)}, u32[]{:S(2)}) async-start(bf16[128,2,640]{2,1,0:T(2,128)(2,1)} %maximum_maximum_fusion), calls=%async_computation | async-start | bytes 655360 | tf_op jit(solution)/shard_map/all_to_all | solution.py:115
  75.2 10.3 %copy-start.3 = (bf16[512,256]{1,0:T(8,128)(2,1)S(1)}, bf16[512,256]{1,0:T(8,128)(2,1)}, u32[]{:S(2)}) copy-start(bf16[512,256]{1,0:T(8,128)(2,1)} %basis_ref.1) | copy-start | bytes 786436
  75.2 242.2 %all-to-all-start.1 = ((bf16[256,128,256]{2,1,0:T(8,128)(2,1)}), bf16[256,128,256]{2,1,0:T(8,128)(2,1)}, u32[]{:S(2)}, u32[]{:S(2)}) async-start(bf16[256,128,256]{2,1,0:T(8,128)(2,1)} %copy.35), calls=%async_computation.1 | async-start | bytes 33554432 | tf_op jit(solution)/shard_map/all_to_all | solution.py:72
  85.6 257.5 %copy-start.2 = (bf16[512,256]{0,1:T(8,128)(2,1)}, bf16[512,256]{0,1:T(8,128)(2,1)S(1)}, u32[]{:S(2)}) copy-start(bf16[512,256]{0,1:T(8,128)(2,1)S(1)} %copy.37) | copy-start | bytes 786436
  317.4 70.7 %copy-start.1 = (f32[8,512]{1,0:T(8,128)S(1)}, f32[8,512]{1,0:T(8,128)}, u32[]{:S(2)}) copy-start(f32[8,512]{1,0:T(8,128)} %param.9) | copy-start | bytes 49156

commit v3 on v2

--- a/solution.py
+++ b/solution.py
@@ -16,11 +16,9 @@
 
 
 def tile_kernel(weight_ref, exchange_ref, basis_t_ref, basis_ref, inner_t_ref, out_ref):
-    left = basis_t_ref[...].astype(jnp.float32) * weight_ref[0]
-    left_high, left_low = split_bf16(left)
-    basis = basis_ref[...]
-    acc = jnp.dot(left_high, basis, preferred_element_type=jnp.float32)
-    acc += jnp.dot(left_low, basis, preferred_element_type=jnp.float32)
+    weight_col = jnp.broadcast_to(weight_ref[0], (8, weight_ref.shape[2])).T[:, 0:1]
+    scaled = (weight_col * basis_ref[...].astype(jnp.float32)).astype(jnp.bfloat16)
+    acc = jnp.dot(basis_t_ref[...], scaled, preferred_element_type=jnp.float32)
     exchange_high, exchange_low = split_bf16(exchange_ref[0])
     inner_t = inner_t_ref[...]
     acc += jnp.dot(inner_t, exchange_high, preferred_element_type=jnp.float32)
@@ -71,8 +69,15 @@
     ).astype(jnp.bfloat16)
     received_exchange = lax.all_to_all(slot_exchange, ("prow", "pcol"), 0, 0, tiled=True)
 
-    all_orbitals = lax.all_gather(orbitals, "pcol", axis=0, tiled=True)
-    orb_count = all_orbitals.shape[0]
+    orb_local = orbitals.shape[0]
+    orb_count = orb_local * col_devs
+    placed_orbitals = lax.dynamic_update_slice_in_dim(
+        jnp.zeros((orb_count, orbitals.shape[1]), orbitals.dtype),
+        orbitals,
+        lax.axis_index("pcol") * orb_local,
+        0,
+    )
+    all_orbitals = lax.psum(placed_orbitals, "pcol")
     channels = jnp.arange(chan_count, dtype=jnp.int32)
     orb_ids = jnp.arange(orb_count, dtype=jnp.int32)
     first_orb = jnp.sum(

time: 395 us -> 474 us (1.20)
  waiting for transfers between devices: 230 us -> 309 us
  blocking collectives: 18.1 us -> 0 us
  between operations: 0.13 us -> 13.5 us
  Pallas kernels: 45.1 us -> 50.6 us
    psum x0 -> x1, waiting for transfers between devices: none -> 79.2 us  [on_device(): all_orbitals = lax.psum(placed_orbitals, 'pcol')]
    all_gather x1 -> x0, blocking collectives: 18.1 us -> none  [on_device(): all_orbitals = lax.all_gather(orbitals, 'pcol', axis=0, tiled=True)]
    pallas_call x1, Pallas kernels: 45.1 us -> 50.6 us  [build_blocks(): pl.pallas_call(tile_kernel, grid=(block_count,), in_specs=[pl.BlockSpec((...]
  transfers between devices with their start and end apart: 2 -> 3, of which waited for: 1 -> 2; matrix products, arithmetic and copies ran while one was open for 10% -> 9% of each run, Pallas kernels for 0% -> 0%
where the time goes in v3:
time: 474 us; the launch traced here: 468 us
  waiting for transfers between devices  309 us (65%)
  Pallas kernels  50.6 us (11%)
  matrix products  39.3 us (8%)
  local copies, waits for them, and re-layouts  31.1 us (7%)
  starting transfers between devices  20.9 us (4%)
  between operations  13.5 us (3%)
    all_to_all x1, waiting for transfers between devices, on_device(): lax.all_to_all(slot_exchange, ('prow', 'pcol'), 0, 0, tiled=True)  230 us
    psum x1, waiting for transfers between devices, on_device(): all_orbitals = lax.psum(placed_orbitals, 'pcol')  79.2 us
    pallas_call x1, Pallas kernels, build_blocks(): pl.pallas_call(tile_kernel, grid=(block_count,), in_specs=[pl.BlockSpec((...  50.6 us
    convert_element_type x1, local copies, waits for them, and re-layouts, on_device(): slot_exchange = jnp.einsum('st,tqb->sqb', matches.astype(jnp.bfloat16), e...  17.9 us
    dot_general x1, matrix products, on_device(): jnp.einsum('st,tqb->sqb', matches.astype(jnp.bfloat16), exchange_ops, pre...  17.8 us
    dot_general x1, matrix products, on_device(): jnp.einsum('gs,sqb->gqb', select, received_exchange, preferred_element_ty...  17.6 us
    all_to_all x1, starting transfers between devices, on_device(): received_small = lax.all_to_all(small, ('prow', 'pcol'), 0, 0, tiled=True)  10.6 us
    all_to_all x1, starting transfers between devices, on_device(): lax.all_to_all(slot_exchange, ('prow', 'pcol'), 0, 0, tiled=True)  10.2 us
  transfers between devices with their start and end apart: 3, of which 2 were waited for; matrix products, arithmetic and copies ran while one was open for 9% of the time, Pallas kernels for 0%

profile of v3, /device:TPU:23, one launch (start us, length us, event | category | flops | bytes accessed | tf_op | source)
XLA Modules:
  0.0 467.5 jit_solution(10139914421185052247)
XLA Ops:
  6.5 0.0 copy-start
  6.5 0.0 all-reduce.2.cloned.1.call-start
  6.5 0.7 constant_dynamic-update-slice_fusion
  7.3 0.0 copy-start.4
  7.3 0.6 copy-done.4
  7.9 0.0 all-reduce.2.cloned.1.call-update
  7.9 0.8 fusion.25
  8.7 0.8 fusion.26
  9.5 0.8 select_reduce_fusion
  10.3 0.2 convert_element_type.51
  10.6 0.1 pad.2.clone
  10.6 0.9 select_reduce_fusion.1
  11.6 79.2 %all-reduce.2.cloned.1.call-done = bf16[64,512]{1,0:T(8,128)(2,1)} async-done(((bf16[64,512]{1,0:T(8,128)(2,1)}), bf16[64,512]{1,0:T(8,128)(2,1)}) %all-reduce.2.cloned.1.call-update) | async-done | bytes 65552 | tf_op jit(solution)/shard_map/psum | solution.py:80
  90.8 1.1 fusion.15
  91.9 1.1 fusion.8
  93.0 0.0 copy-done
  93.0 0.4 fusion.7
  93.4 1.2 convolution_convert_fusion
  94.6 0.1 concatenate.6
  94.7 1.1 maximum_maximum_fusion
  95.8 10.6 %all-to-all-start = ((bf16[128,2,640]{2,1,0:T(2,128)(2,1)}), bf16[128,2,640]{2,1,0:T(2,128)(2,1)S(1)}, u32[]{:S(2)}, u32[]{:S(2)}) async-start(bf16[128,2,640]{2,1,0:T(2,128)(2,1)} %maximum_maximum_fusion), calls=%async_computation | async-start | bytes 655360 | tf_op jit(solution)/shard_map/all_to_all | solution.py:120
  106.4 17.8 %fusion.4 = bf16[256,128,256]{2,0,1:T(8,128)(2,1)} fusion(bf16[192,128,256]{2,1,0:T(8,128)(2,1)} %param.15, s32[192]{0:T(256)} %param.13), kind=kOutput, calls=%fused_computation.4 | convolution fusion | flops 3229663232 | bytes 29360896 | tf_op jit(solution)/shard_map/st,tqb->sqb/dot_general | solution.py:64
  124.2 17.9 %copy.35 = bf16[256,128,256]{2,1,0:T(8,128)(2,1)} copy(bf16[256,128,256]{2,0,1:T(8,128)(2,1)} %fusion.4) | data formatting | bytes 33554432 | tf_op jit(solution)/shard_map/convert_element_type | solution.py:69
  142.2 0.0 copy-start.3
  142.2 0.0 all-to-all-done
  142.2 10.2 %all-to-all-start.1 = ((bf16[256,128,256]{2,1,0:T(8,128)(2,1)}), bf16[256,128,256]{2,1,0:T(8,128)(2,1)}, u32[]{:S(2)}, u32[]{:S(2)}) async-start(bf16[256,128,256]{2,1,0:T(8,128)(2,1)} %copy.35), calls=%async_computation.1 | async-start | bytes 33554432 | tf_op jit(solution)/shard_map/all_to_all | solution.py:70
  152.4 0.0 copy-done.3
  152.4 0.1 copy.37
  152.6 0.0 copy-start.2
  152.6 0.7 slice_bitcast_fusion.inner_t_ref
  153.3 0.1 all_to_all.10
  153.4 0.1 convert_reduce_fusion
  153.5 0.2 fusion.9
  153.7 0.7 reshape.115.weight_ref
  154.4 229.9 %all-to-all-done.1 = bf16[256,128,256]{2,1,0:T(8,128)(2,1)} async-done(((bf16[256,128,256]{2,1,0:T(8,128)(2,1)}), bf16[256,128,256]{2,1,0:T(8,128)(2,1)}, u32[]{:S(2)}, u32[]{:S(2)}) %all-to-all-start.1) | async-done | bytes 16777248 | tf_op jit(solution)/shard_map/all_to_all | solution.py:70
  384.4 0.0 copy-start.1
  384.4 17.6 %fusion = f32[64,128,256]{2,0,1:T(8,128)S(1)} fusion(bf16[256,128,256]{2,1,0:T(8,128)(2,1)} %all-to-all-done.1, s32[256]{0:T(256)S(1)} %convert_reduce_fusion), kind=kOutput, calls=%fused_computation | convolution fusion | flops 1073758208 | bytes 25166848 | tf_op jit(solution)/shard_map/gs,sqb->gqb/dot_general | solution.py:129
  402.0 8.1 %copy.39.exchange_ref = f32[64,128,256]{2,1,0:T(8,128)} copy(f32[64,128,256]{2,0,1:T(8,128)S(1)} %fusion) | data formatting | bytes 16777216 | tf_op jit(solution)/shard_map/gs,sqb->gqb/dot_general | solution.py:129
  410.0 0.0 copy-done.2
  410.0 50.6 %shard_map.82 = bf16[64,256,256]{2,1,0:T(8,128)(2,1)} custom-call(f32[64,1,512]{2,1,0:T(1,128)} %reshape.115.weight_ref, f32[64,128,256]{2,1,0:T(8,128)} %copy.39.exchange_ref, bf16[256,512]{1,0:T(8,128)(2,1)} %bitcast.21, bf16[512,256]{1,0:T(8,128)(2,1)} %basis_ref.1, bf16[256,128]{1,0:T(8,128)(2,1)} %slice_bitcast_fusion.inner_t_ref), custom_call_target="tpu_custom_call" | custom-call | tf_op jit(solution)/shard_map/pallas_call | solution.py:34
  460.7 0.0 copy-done.1
  (4 shorter events, 0.0 us)
Async XLA Ops:
  6.5 86.5 %copy-start = (f32[8,512]{1,0:T(8,128)S(1)}, f32[8,512]{1,0:T(8,128)}, u32[]{:S(2)}) copy-start(f32[8,512]{1,0:T(8,128)} %param.9) | copy-start | bytes 49156
  6.5 84.3 %all-reduce.2.cloned.1.call-start = ((), (), s32[]{:S(2)}) async-start(), calls=%async_computation.2 | async-start | bytes 131072 | tf_op jit(solution)/shard_map/psum | solution.py:80
  7.3 0.6 copy-start.4
  95.8 46.4 %all-to-all-start = ((bf16[128,2,640]{2,1,0:T(2,128)(2,1)}), bf16[128,2,640]{2,1,0:T(2,128)(2,1)S(1)}, u32[]{:S(2)}, u32[]{:S(2)}) async-start(bf16[128,2,640]{2,1,0:T(2,128)(2,1)} %maximum_maximum_fusion), calls=%async_computation | async-start | bytes 655360 | tf_op jit(solution)/shard_map/all_to_all | solution.py:120
  142.2 10.3 %copy-start.3 = (bf16[512,256]{1,0:T(8,128)(2,1)S(1)}, bf16[512,256]{1,0:T(8,128)(2,1)}, u32[]{:S(2)}) copy-start(bf16[512,256]{1,0:T(8,128)(2,1)} %basis_ref.1) | copy-start | bytes 786436
  142.2 242.2 %all-to-all-start.1 = ((bf16[256,128,256]{2,1,0:T(8,128)(2,1)}), bf16[256,128,256]{2,1,0:T(8,128)(2,1)}, u32[]{:S(2)}, u32[]{:S(2)}) async-start(bf16[256,128,256]{2,1,0:T(8,128)(2,1)} %copy.35), calls=%async_computation.1 | async-start | bytes 33554432 | tf_op jit(solution)/shard_map/all_to_all | solution.py:70
  152.6 257.5 %copy-start.2 = (bf16[512,256]{0,1:T(8,128)(2,1)}, bf16[512,256]{0,1:T(8,128)(2,1)S(1)}, u32[]{:S(2)}) copy-start(bf16[512,256]{0,1:T(8,128)(2,1)S(1)} %copy.37) | copy-start | bytes 786436
  384.4 76.3 %copy-start.1 = (f32[8,512]{1,0:T(8,128)S(1)}, f32[8,512]{1,0:T(8,128)}, u32[]{:S(2)}) copy-start(f32[8,512]{1,0:T(8,128)} %param.9) | copy-start | bytes 49156
Sparse Core Ops, SparseCore 0:
  10.6 80.2 all-reduce.1

commit v4 on v2

--- a/solution.py
+++ b/solution.py
@@ -16,36 +16,36 @@
 
 
 def tile_kernel(weight_ref, exchange_ref, basis_t_ref, basis_ref, inner_t_ref, out_ref):
-    left = basis_t_ref[...].astype(jnp.float32) * weight_ref[0]
-    left_high, left_low = split_bf16(left)
+    basis_t = basis_t_ref[...]
     basis = basis_ref[...]
-    acc = jnp.dot(left_high, basis, preferred_element_type=jnp.float32)
-    acc += jnp.dot(left_low, basis, preferred_element_type=jnp.float32)
-    exchange_high, exchange_low = split_bf16(exchange_ref[0])
     inner_t = inner_t_ref[...]
-    acc += jnp.dot(inner_t, exchange_high, preferred_element_type=jnp.float32)
-    acc += jnp.dot(inner_t, exchange_low, preferred_element_type=jnp.float32)
-    out_ref[0] = acc.astype(out_ref.dtype)
+    for j in range(out_ref.shape[0]):
+        left = (basis_t * weight_ref[j : j + 1, :]).astype(jnp.bfloat16)
+        acc = jnp.dot(left, basis, preferred_element_type=jnp.float32)
+        exchange_high, exchange_low = split_bf16(exchange_ref[:, j, :])
+        acc += jnp.dot(inner_t, exchange_high, preferred_element_type=jnp.float32)
+        acc += jnp.dot(inner_t, exchange_low, preferred_element_type=jnp.float32)
+        out_ref[j] = acc.astype(out_ref.dtype)
 
 
-def build_blocks(weight_sum, exchange_sum, basis):
+def build_blocks(weight_sum, exchange_sum, basis, group=8):
     block_count, point_count = weight_sum.shape
-    inner_count, spline_count = exchange_sum.shape[1:]
-    basis_t = basis.T
+    inner_count, _, spline_count = exchange_sum.shape
+    basis_t = basis.T.astype(jnp.float32)
     inner_t = basis[:inner_count].T
     return pl.pallas_call(
         tile_kernel,
-        grid=(block_count,),
+        grid=(block_count // group,),
         in_specs=[
-            pl.BlockSpec((1, 1, point_count), lambda g: (g, 0, 0)),
-            pl.BlockSpec((1, inner_count, spline_count), lambda g: (g, 0, 0)),
+            pl.BlockSpec((group, point_count), lambda g: (g, 0)),
+            pl.BlockSpec((inner_count, group, spline_count), lambda g: (0, g, 0)),
             pl.BlockSpec((spline_count, point_count), lambda g: (0, 0)),
             pl.BlockSpec((point_count, spline_count), lambda g: (0, 0)),
             pl.BlockSpec((spline_count, inner_count), lambda g: (0, 0)),
         ],
-        out_specs=pl.BlockSpec((1, spline_count, spline_count), lambda g: (g, 0, 0)),
+        out_specs=pl.BlockSpec((group, spline_count, spline_count), lambda g: (g, 0, 0)),
         out_shape=jax.ShapeDtypeStruct((block_count, spline_count, spline_count), jnp.bfloat16),
-    )(weight_sum.reshape(block_count, 1, point_count), exchange_sum, basis_t, basis, inner_t)
+    )(weight_sum, exchange_sum, basis_t, basis, inner_t)
 
 
 def on_device(basis, potentials, orbitals, chan_orbital, pair_list, slot_list, coefs, exchange_ops):
@@ -122,7 +122,7 @@
         select, received_small[:, :point_count], preferred_element_type=jnp.float32
     )
     exchange_sum = jnp.einsum(
-        "gs,sqb->gqb", select, received_exchange, preferred_element_type=jnp.float32
+        "gs,sqb->qgb", select, received_exchange, preferred_element_type=jnp.float32
     )
     blocks = build_blocks(weight_sum, exchange_sum, basis)
     return blocks.reshape(RBLK, 1, BAND, 1, spline_count, spline_count)

time: 395 us -> 376 us (0.952)
  Pallas kernels: 45.1 us -> 34.6 us
  local copies, waits for them, and re-layouts: 29.7 us -> 20.8 us
    pallas_call x1, Pallas kernels: 45.1 us -> 34.6 us  [build_blocks(): pl.pallas_call(tile_kernel, grid=(block_count // group,), in_specs=[pl.Bl...]
    dot_general x1 -> x0, local copies, waits for them, and re-layouts: 8.08 us -> none  [on_device(): jnp.einsum('gs,sqb->gqb', select, received_exchange, preferred_element_ty...]
where the time goes in v4:
time: 376 us; the launch traced here: 371 us
  waiting for transfers between devices  229 us (61%)
  matrix products  39.6 us (11%)
  Pallas kernels  34.6 us (9%)
  starting transfers between devices  24.5 us (7%)
  local copies, waits for them, and re-layouts  20.8 us (6%)
  blocking collectives  18.1 us (5%)
  other arithmetic  3.83 us (1%)
    all_to_all x1, waiting for transfers between devices, on_device(): lax.all_to_all(slot_exchange, ('prow', 'pcol'), 0, 0, tiled=True)  229 us
    pallas_call x1, Pallas kernels, build_blocks(): pl.pallas_call(tile_kernel, grid=(block_count // group,), in_specs=[pl.Bl...  34.6 us
    dot_general x1, matrix products, on_device(): jnp.einsum('gs,sqb->qgb', select, received_exchange, preferred_element_ty...  18.9 us
    all_gather x1, blocking collectives, on_device(): all_orbitals = lax.all_gather(orbitals, 'pcol', axis=0, tiled=True)  18.1 us
    convert_element_type x1, local copies, waits for them, and re-layouts, on_device(): slot_exchange = jnp.einsum('st,tqb->sqb', matches.astype(jnp.bfloat16), e...  17.9 us
    dot_general x1, matrix products, on_device(): jnp.einsum('st,tqb->sqb', matches.astype(jnp.bfloat16), exchange_ops, pre...  17.8 us
    all_to_all x1, starting transfers between devices, on_device(): received_small = lax.all_to_all(small, ('prow', 'pcol'), 0, 0, tiled=True)  14.3 us
    all_to_all x1, starting transfers between devices, on_device(): lax.all_to_all(slot_exchange, ('prow', 'pcol'), 0, 0, tiled=True)  10.2 us
  transfers between devices with their start and end apart: 2, of which 1 were waited for; matrix products, arithmetic and copies ran while one was open for 10% of the time, Pallas kernels for 0%

profile of v4, /device:TPU:23, one launch (start us, length us, event | category | flops | bytes accessed | tf_op | source)
XLA Modules:
  0.0 370.9 jit_solution(1633954507995425647)
XLA Ops:
  0.0 0.0 copy-start
  0.0 0.8 fusion.28
  0.8 0.9 select_reduce_fusion.1
  1.8 18.1 %all-gather = bf16[16,4,512]{2,1,0:T(4,128)(2,1)S(1)} all-gather(bf16[1,4,512]{2,1,0:T(4,128)(2,1)} %bitcast.32), channel_id=1, replica_groups=mesh['prow'=8,'pcol'=16] {'pcol'}, dimensions={0}, use_global_device_ids=true | all-gather | bytes 69632 | tf_op jit(solution)/shard_map/all_gather | solution.py:74
  19.9 0.8 fusion.29
  20.7 0.2 fusion.18
  20.9 0.3 fusion.11
  21.2 0.0 copy-done
  21.2 0.4 fusion.10
  21.6 1.2 convolution_convert_fusion
  22.7 0.1 concatenate.6
  22.9 0.8 select_reduce_fusion
  23.7 0.2 convert_element_type.59
  23.9 0.1 pad.2.clone
  24.0 1.1 maximum_maximum_fusion
  25.1 14.3 %all-to-all-start = ((bf16[128,2,640]{2,1,0:T(2,128)(2,1)}), bf16[128,2,640]{2,1,0:T(2,128)(2,1)S(1)}, u32[]{:S(2)}, u32[]{:S(2)}) async-start(bf16[128,2,640]{2,1,0:T(2,128)(2,1)} %maximum_maximum_fusion), calls=%async_computation | async-start | bytes 655360 | tf_op jit(solution)/shard_map/all_to_all | solution.py:115
  39.4 17.8 %fusion.4 = bf16[256,128,256]{2,0,1:T(8,128)(2,1)} fusion(bf16[192,128,256]{2,1,0:T(8,128)(2,1)} %param.15, s32[192]{0:T(256)} %param.13), kind=kOutput, calls=%fused_computation.4 | convolution fusion | flops 3229663232 | bytes 29360896 | tf_op jit(solution)/shard_map/st,tqb->sqb/dot_general | solution.py:66
  57.3 17.9 %copy.31 = bf16[256,128,256]{2,1,0:T(8,128)(2,1)} copy(bf16[256,128,256]{2,0,1:T(8,128)(2,1)} %fusion.4) | data formatting | bytes 33554432 | tf_op jit(solution)/shard_map/convert_element_type | solution.py:71
  75.2 0.0 copy-start.2
  75.2 0.0 all-to-all-done
  75.2 10.2 %all-to-all-start.1 = ((bf16[256,128,256]{2,1,0:T(8,128)(2,1)}), bf16[256,128,256]{2,1,0:T(8,128)(2,1)}, u32[]{:S(2)}, u32[]{:S(2)}) async-start(bf16[256,128,256]{2,1,0:T(8,128)(2,1)} %copy.31), calls=%async_computation.1 | async-start | bytes 33554432 | tf_op jit(solution)/shard_map/all_to_all | solution.py:72
  85.4 0.0 copy-done.2
  85.4 0.1 copy.33
  85.6 0.6 slice_bitcast_fusion.inner_t_ref
  86.2 0.9 convert_bitcast_fusion.basis_t_ref
  87.1 0.1 all_to_all.10
  87.2 0.1 convert_reduce_fusion
  87.3 0.8 fusion.12.weight_ref
  88.1 229.3 %all-to-all-done.1 = bf16[256,128,256]{2,1,0:T(8,128)(2,1)} async-done(((bf16[256,128,256]{2,1,0:T(8,128)(2,1)}), bf16[256,128,256]{2,1,0:T(8,128)(2,1)}, u32[]{:S(2)}, u32[]{:S(2)}) %all-to-all-start.1) | async-done | bytes 16777248 | tf_op jit(solution)/shard_map/all_to_all | solution.py:72
  317.4 0.0 copy-start.1
  317.4 18.9 %fusion.7.exchange_ref = f32[128,64,256]{2,1,0:T(8,128)} fusion(bf16[256,128,256]{2,1,0:T(8,128)(2,1)} %all-to-all-done.1, s32[256]{0:T(256)S(1)} %convert_reduce_fusion), kind=kOutput, calls=%fused_computation.5 | convolution fusion | flops 1073758208 | bytes 25166848 | tf_op jit(solution)/shard_map/gs,sqb->qgb/dot_general | solution.py:124
  336.3 34.6 %shard_map.82 = bf16[64,256,256]{2,1,0:T(8,128)(2,1)} custom-call(f32[64,512]{1,0:T(8,128)} %fusion.12.weight_ref, f32[128,64,256]{2,1,0:T(8,128)} %fusion.7.exchange_ref, f32[256,512]{1,0:T(8,128)} %convert_bitcast_fusion.basis_t_ref, bf16[512,256]{1,0:T(8,128)(2,1)} %basis_ref.1, bf16[256,128]{1,0:T(8,128)(2,1)} %slice_bitcast_fusion.inner_t_ref), custom_call_target="tpu_custom_call" | custom-call | tf_op jit(solution)/shard_map/pallas_call | solution.py:36
  370.9 0.0 copy-done.1
  (4 shorter events, 0.1 us)
Async XLA Ops:
  0.0 21.2 %copy-start = (f32[8,512]{1,0:T(8,128)S(1)}, f32[8,512]{1,0:T(8,128)}, u32[]{:S(2)}) copy-start(f32[8,512]{1,0:T(8,128)} %param.9) | copy-start | bytes 49156
  25.1 50.1 %all-to-all-start = ((bf16[128,2,640]{2,1,0:T(2,128)(2,1)}), bf16[128,2,640]{2,1,0:T(2,128)(2,1)S(1)}, u32[]{:S(2)}, u32[]{:S(2)}) async-start(bf16[128,2,640]{2,1,0:T(2,128)(2,1)} %maximum_maximum_fusion), calls=%async_computation | async-start | bytes 655360 | tf_op jit(solution)/shard_map/all_to_all | solution.py:115
  75.2 10.3 %copy-start.2 = (bf16[512,256]{1,0:T(8,128)(2,1)S(1)}, bf16[512,256]{1,0:T(8,128)(2,1)}, u32[]{:S(2)}) copy-start(bf16[512,256]{1,0:T(8,128)(2,1)} %basis_ref.1) | copy-start | bytes 786436
  75.2 242.2 %all-to-all-start.1 = ((bf16[256,128,256]{2,1,0:T(8,128)(2,1)}), bf16[256,128,256]{2,1,0:T(8,128)(2,1)}, u32[]{:S(2)}, u32[]{:S(2)}) async-start(bf16[256,128,256]{2,1,0:T(8,128)(2,1)} %copy.31), calls=%async_computation.1 | async-start | bytes 33554432 | tf_op jit(solution)/shard_map/all_to_all | solution.py:72
  317.4 53.5 %copy-start.1 = (f32[8,512]{1,0:T(8,128)S(1)}, f32[8,512]{1,0:T(8,128)}, u32[]{:S(2)}) copy-start(f32[8,512]{1,0:T(8,128)} %param.9) | copy-start | bytes 49156

commit v5 on v4

--- a/solution.py
+++ b/solution.py
@@ -71,56 +71,66 @@
     ).astype(jnp.bfloat16)
     received_exchange = lax.all_to_all(slot_exchange, ("prow", "pcol"), 0, 0, tiled=True)
 
-    all_orbitals = lax.all_gather(orbitals, "pcol", axis=0, tiled=True)
-    orb_count = all_orbitals.shape[0]
     channels = jnp.arange(chan_count, dtype=jnp.int32)
-    orb_ids = jnp.arange(orb_count, dtype=jnp.int32)
     first_orb = jnp.sum(
         jnp.where(first_chan[:, None] == channels[None, :], chan_orbital[None, :], 0), axis=1
     )
     second_orb = jnp.sum(
         jnp.where(second_chan[:, None] == channels[None, :], chan_orbital[None, :], 0), axis=1
     )
-    first_rows = jnp.dot(
-        (first_orb[:, None] == orb_ids[None, :]).astype(jnp.bfloat16),
-        all_orbitals,
-        preferred_element_type=jnp.float32,
-    )
-    second_rows = jnp.dot(
-        (second_orb[:, None] == orb_ids[None, :]).astype(jnp.bfloat16),
-        all_orbitals,
-        preferred_element_type=jnp.float32,
-    )
+    match_float = matches.astype(jnp.float32)
     pick_pot = (
         multipole[:, None] == jnp.arange(potentials.shape[0], dtype=jnp.int32)[None, :]
     ).astype(jnp.float32)
-    pot_rows = jnp.dot(pick_pot, potentials, precision=lax.Precision.HIGHEST)
-    radial = coefs[:, 0:1] * pot_rows + coefs[:, 1:2] * (first_rows * second_rows)
-    slot_weight = jnp.dot(
-        matches.astype(jnp.float32), radial, precision=lax.Precision.HIGHEST
-    ).astype(jnp.bfloat16)
+    slot_pot_coef = jnp.dot(
+        match_float * coefs[None, :, 0], pick_pot, precision=lax.Precision.HIGHEST
+    )
+    slot_pot = jnp.dot(slot_pot_coef, potentials, precision=lax.Precision.HIGHEST)
+    slot_orb_coef = jnp.dot(match_float, coefs[:, 1], precision=lax.Precision.HIGHEST)
     offset = jnp.mod(second_chan // col_devs - first_chan // col_devs, col_groups)
     block_index = first_chan // row_devs * BAND + offset
-    slot_ids = jnp.max(jnp.where(matches, block_index[None, :], -1), axis=1)
 
-    width = -(-(point_count + 1) // 128) * 128
+    def per_slot(values):
+        return jnp.max(jnp.where(matches, values[None, :], -1), axis=1).astype(jnp.float32)
+
+    tail = jnp.stack(
+        [slot_orb_coef, per_slot(first_orb), per_slot(second_orb), per_slot(block_index)], axis=1
+    )
+    width = -(-(point_count + tail.shape[1]) // 128) * 128
     small = jnp.concatenate(
         [
-            slot_weight,
-            slot_ids.astype(jnp.bfloat16)[:, None],
-            jnp.zeros((slot_count, width - point_count - 1), jnp.bfloat16),
+            slot_pot,
+            tail,
+            jnp.zeros((slot_count, width - point_count - tail.shape[1]), jnp.float32),
         ],
         axis=1,
     )
     received_small = lax.all_to_all(small, ("prow", "pcol"), 0, 0, tiled=True)
 
-    idents = received_small[:, point_count].astype(jnp.float32).astype(jnp.int32)
+    all_orbitals = lax.all_gather(orbitals, "pcol", axis=0, tiled=True)
+    orb_ids = jnp.arange(all_orbitals.shape[0], dtype=jnp.int32)
+    recv_first = received_small[:, point_count + 1].astype(jnp.int32)
+    recv_second = received_small[:, point_count + 2].astype(jnp.int32)
+    idents = received_small[:, point_count + 3].astype(jnp.int32)
+    first_rows = jnp.dot(
+        (recv_first[:, None] == orb_ids[None, :]).astype(jnp.bfloat16),
+        all_orbitals,
+        preferred_element_type=jnp.float32,
+    )
+    second_rows = jnp.dot(
+        (recv_second[:, None] == orb_ids[None, :]).astype(jnp.bfloat16),
+        all_orbitals,
+        preferred_element_type=jnp.float32,
+    )
+    slot_weight = (
+        received_small[:, :point_count]
+        + received_small[:, point_count : point_count + 1] * (first_rows * second_rows)
+    ).astype(jnp.bfloat16)
+
     select = (jnp.arange(block_count, dtype=jnp.int32)[:, None] == idents[None, :]).astype(
         jnp.bfloat16
     )
-    weight_sum = jnp.dot(
-        select, received_small[:, :point_count], preferred_element_type=jnp.float32
-    )
+    weight_sum = jnp.dot(select, slot_weight, preferred_element_type=jnp.float32)
     exchange_sum = jnp.einsum(
         "gs,sqb->qgb", select, received_exchange, preferred_element_type=jnp.float32
     )

time: 376 us -> 364 us (0.968); the launches traced: 371 us -> 363 us
  waiting for transfers between devices: 229 us -> 13.4 us
  blocking collectives: 18.1 us -> 226 us
  local copies, waits for them, and re-layouts: 20.8 us -> 25.2 us
    all_to_all x1, waiting for transfers between devices: 229 us -> 13.4 us  [on_device(): lax.all_to_all(slot_exchange, ('prow', 'pcol'), 0, 0, tiled=True)]
    all_gather x1, blocking collectives: 18.1 us -> 226 us  [on_device(): all_orbitals = lax.all_gather(orbitals, 'pcol', axis=0, tiled=True)]
  transfers between devices with their start and end apart: 2 -> 2, of which waited for: 1 -> 1; matrix products, arithmetic and copies ran while one was open for 10% -> 11% of each run, Pallas kernels for 0% -> 0%
where the time goes in v5:
time: 364 us; the launch traced here: 363 us
  blocking collectives  226 us (62%)
  matrix products  39.7 us (11%)
  Pallas kernels  34.6 us (10%)
  local copies, waits for them, and re-layouts  25.2 us (7%)
  starting transfers between devices  20.8 us (6%)
  waiting for transfers between devices  13.4 us (4%)
  other arithmetic  4.06 us (1%)
    all_gather x1, blocking collectives, on_device(): all_orbitals = lax.all_gather(orbitals, 'pcol', axis=0, tiled=True)  226 us
    pallas_call x1, Pallas kernels, build_blocks(): pl.pallas_call(tile_kernel, grid=(block_count // group,), in_specs=[pl.Bl...  34.6 us
    dot_general x1, matrix products, on_device(): jnp.einsum('gs,sqb->qgb', select, received_exchange, preferred_element_ty...  18.9 us
    convert_element_type x1, local copies, waits for them, and re-layouts, on_device(): slot_exchange = jnp.einsum('st,tqb->sqb', matches.astype(jnp.bfloat16), e...  17.9 us
    dot_general x1, matrix products, on_device(): jnp.einsum('st,tqb->sqb', matches.astype(jnp.bfloat16), exchange_ops, pre...  17.8 us
    all_to_all x1, waiting for transfers between devices, on_device(): lax.all_to_all(slot_exchange, ('prow', 'pcol'), 0, 0, tiled=True)  13.4 us
    all_to_all x1, starting transfers between devices, on_device(): received_small = lax.all_to_all(small, ('prow', 'pcol'), 0, 0, tiled=True)  10.6 us
    all_to_all x1, starting transfers between devices, on_device(): lax.all_to_all(slot_exchange, ('prow', 'pcol'), 0, 0, tiled=True)  10.2 us
  transfers between devices with their start and end apart: 2, of which 1 were waited for; matrix products, arithmetic and copies ran while one was open for 11% of the time, Pallas kernels for 0%

profile of v5, /device:TPU:23, one launch (start us, length us, event | category | flops | bytes accessed | tf_op | source)
XLA Modules:
  0.0 363.4 jit_solution(16321866571607083388)
XLA Ops:
  0.0 0.0 copy-start
  0.0 0.8 fusion.41
  0.8 0.8 fusion.40
  1.6 1.0 fusion.17
  2.6 0.0 copy-done
  2.6 0.6 fusion.42
  3.2 0.3 concatenate.6
  3.5 1.0 fusion.15
  4.6 0.9 copy.38
  5.5 0.9 select_reduce_fusion.2
  6.4 0.9 select_reduce_fusion
  7.3 0.3 convert_element_type.92
  7.6 0.3 convert_element_type.93
  7.9 0.3 convert_element_type.94
  8.2 2.3 concatenate.7
  10.5 10.6 %all-to-all-start = ((f32[128,2,640]{2,1,0:T(2,128)}), f32[128,2,640]{2,1,0:T(2,128)S(1)}, u32[]{:S(2)}, u32[]{:S(2)}) async-start(f32[128,2,640]{2,1,0:T(2,128)} %concatenate.7), calls=%async_computation | async-start | bytes 1310720 | tf_op jit(solution)/shard_map/all_to_all | solution.py:108
  21.1 17.8 %fusion.4 = bf16[256,128,256]{2,0,1:T(8,128)(2,1)} fusion(bf16[192,128,256]{2,1,0:T(8,128)(2,1)} %param.15, s32[192]{0:T(256)} %param.13), kind=kOutput, calls=%fused_computation.4 | convolution fusion | flops 3229663232 | bytes 29360896 | tf_op jit(solution)/shard_map/st,tqb->sqb/dot_general | solution.py:66
  38.9 17.9 %copy.43 = bf16[256,128,256]{2,1,0:T(8,128)(2,1)} copy(bf16[256,128,256]{2,0,1:T(8,128)(2,1)} %fusion.4) | data formatting | bytes 33554432 | tf_op jit(solution)/shard_map/convert_element_type | solution.py:71
  56.9 0.0 copy-start.3
  56.9 0.0 copy-start.2
  56.9 0.0 all-to-all-done
  56.9 10.2 %all-to-all-start.1 = ((bf16[256,128,256]{2,1,0:T(8,128)(2,1)}), bf16[256,128,256]{2,1,0:T(8,128)(2,1)}, u32[]{:S(2)}, u32[]{:S(2)}) async-start(bf16[256,128,256]{2,1,0:T(8,128)(2,1)} %copy.43), calls=%async_computation.1 | async-start | bytes 33554432 | tf_op jit(solution)/shard_map/all_to_all | solution.py:72
  67.1 0.0 copy-done.3
  67.1 225.5 %all-gather = bf16[16,4,512]{2,1,0:T(4,128)(2,1)S(1)} all-gather(bf16[1,4,512]{2,1,0:T(4,128)(2,1)S(1)} %bitcast.36), channel_id=1, replica_groups=mesh['prow'=8,'pcol'=16] {'pcol'}, dimensions={0}, use_global_device_ids=true | all-gather | bytes 69632 | tf_op jit(solution)/shard_map/all_gather | solution.py:110
  292.6 0.0 copy-done.2
  292.7 0.1 copy.45
  292.8 0.6 slice_bitcast_fusion.inner_t_ref
  293.4 0.9 convert_bitcast_fusion.basis_t_ref
  294.3 0.5 all_to_all.10
  294.7 0.1 slice_reduce_fusion
  294.9 0.3 fusion.23
  295.2 0.3 fusion.24
  295.5 1.1 fusion.13.weight_ref
  296.5 13.4 %all-to-all-done.1 = bf16[256,128,256]{2,1,0:T(8,128)(2,1)} async-done(((bf16[256,128,256]{2,1,0:T(8,128)(2,1)}), bf16[256,128,256]{2,1,0:T(8,128)(2,1)}, u32[]{:S(2)}, u32[]{:S(2)}) %all-to-all-start.1) | async-done | bytes 16777248 | tf_op jit(solution)/shard_map/all_to_all | solution.py:72
  309.9 0.0 copy-start.1
  309.9 18.9 %fusion.7.exchange_ref = f32[128,64,256]{2,1,0:T(8,128)} fusion(bf16[256,128,256]{2,1,0:T(8,128)(2,1)} %all-to-all-done.1, s32[256]{0:T(256)S(1)} %get-tuple-element.5), kind=kOutput, calls=%fused_computation.5 | convolution fusion | flops 1073758208 | bytes 25166848 | tf_op jit(solution)/shard_map/gs,sqb->qgb/dot_general | solution.py:134
  328.8 34.6 %shard_map.82 = bf16[64,256,256]{2,1,0:T(8,128)(2,1)} custom-call(f32[64,512]{1,0:T(8,128)} %fusion.13.weight_ref, f32[128,64,256]{2,1,0:T(8,128)} %fusion.7.exchange_ref, f32[256,512]{1,0:T(8,128)} %convert_bitcast_fusion.basis_t_ref, bf16[512,256]{1,0:T(8,128)(2,1)} %basis_ref.1, bf16[256,128]{1,0:T(8,128)(2,1)} %slice_bitcast_fusion.inner_t_ref), custom_call_target="tpu_custom_call" | custom-call | tf_op jit(solution)/shard_map/pallas_call | solution.py:36
  363.4 0.0 copy-done.1
  (7 shorter events, 0.1 us)
Async XLA Ops:
  0.0 2.6 copy-start
  10.5 46.4 %all-to-all-start = ((f32[128,2,640]{2,1,0:T(2,128)}), f32[128,2,640]{2,1,0:T(2,128)S(1)}, u32[]{:S(2)}, u32[]{:S(2)}) async-start(f32[128,2,640]{2,1,0:T(2,128)} %concatenate.7), calls=%async_computation | async-start | bytes 1310720 | tf_op jit(solution)/shard_map/all_to_all | solution.py:108
  56.9 10.2 %copy-start.3 = (bf16[4,512]{1,0:T(4,128)(2,1)S(1)}, bf16[4,512]{1,0:T(4,128)(2,1)}, u32[]{:S(2)}) copy-start(bf16[4,512]{1,0:T(4,128)(2,1)} %param.10) | copy-start | bytes 12292
  56.9 235.8 %copy-start.2 = (bf16[512,256]{1,0:T(8,128)(2,1)S(1)}, bf16[512,256]{1,0:T(8,128)(2,1)}, u32[]{:S(2)}) copy-start(bf16[512,256]{1,0:T(8,128)(2,1)} %basis_ref.1) | copy-start | bytes 786436
  56.9 253.1 %all-to-all-start.1 = ((bf16[256,128,256]{2,1,0:T(8,128)(2,1)}), bf16[256,128,256]{2,1,0:T(8,128)(2,1)}, u32[]{:S(2)}, u32[]{:S(2)}) async-start(bf16[256,128,256]{2,1,0:T(8,128)(2,1)} %copy.43), calls=%async_computation.1 | async-start | bytes 33554432 | tf_op jit(solution)/shard_map/all_to_all | solution.py:72
  309.9 53.5 %copy-start.1 = (f32[8,512]{1,0:T(8,128)S(1)}, f32[8,512]{1,0:T(8,128)}, u32[]{:S(2)}) copy-start(f32[8,512]{1,0:T(8,128)} %param.9) | copy-start | bytes 49156

commit v6 on v5

--- a/solution.py
+++ b/solution.py
@@ -2,6 +2,7 @@
 import jax.numpy as jnp
 from jax import lax
 from jax.experimental import pallas as pl
+from jax.experimental.pallas import tpu as pltpu
 from jax.sharding import PartitionSpec as P
 
 CAP = 2
@@ -15,16 +16,19 @@
     return high, low
 
 
-def tile_kernel(weight_ref, exchange_ref, basis_t_ref, basis_ref, inner_t_ref, out_ref):
+def tile_kernel(weight_ref, exchange_ref, basis_t_ref, basis_ref, inner_t_ref, out_ref, lhs_ref, rhs_ref):
+    point_count = basis_ref.shape[0]
+    inner_count = inner_t_ref.shape[1]
+    lhs_ref[:, point_count : point_count + inner_count] = inner_t_ref[...]
+    lhs_ref[:, point_count + inner_count :] = inner_t_ref[...]
+    rhs_ref[:point_count, :] = basis_ref[...]
     basis_t = basis_t_ref[...]
-    basis = basis_ref[...]
-    inner_t = inner_t_ref[...]
     for j in range(out_ref.shape[0]):
-        left = (basis_t * weight_ref[j : j + 1, :]).astype(jnp.bfloat16)
-        acc = jnp.dot(left, basis, preferred_element_type=jnp.float32)
+        lhs_ref[:, :point_count] = (basis_t * weight_ref[j : j + 1, :]).astype(jnp.bfloat16)
         exchange_high, exchange_low = split_bf16(exchange_ref[:, j, :])
-        acc += jnp.dot(inner_t, exchange_high, preferred_element_type=jnp.float32)
-        acc += jnp.dot(inner_t, exchange_low, preferred_element_type=jnp.float32)
+        rhs_ref[point_count : point_count + inner_count, :] = exchange_high
+        rhs_ref[point_count + inner_count :, :] = exchange_low
+        acc = jnp.dot(lhs_ref[...], rhs_ref[...], preferred_element_type=jnp.float32)
         out_ref[j] = acc.astype(out_ref.dtype)
 
 
@@ -33,6 +37,7 @@
     inner_count, _, spline_count = exchange_sum.shape
     basis_t = basis.T.astype(jnp.float32)
     inner_t = basis[:inner_count].T
+    depth = point_count + 2 * inner_count
     return pl.pallas_call(
         tile_kernel,
         grid=(block_count // group,),
@@ -45,6 +50,10 @@
         ],
         out_specs=pl.BlockSpec((group, spline_count, spline_count), lambda g: (g, 0, 0)),
         out_shape=jax.ShapeDtypeStruct((block_count, spline_count, spline_count), jnp.bfloat16),
+        scratch_shapes=[
+            pltpu.VMEM((spline_count, depth), jnp.bfloat16),
+            pltpu.VMEM((depth, spline_count), jnp.bfloat16),
+        ],
     )(weight_sum, exchange_sum, basis_t, basis, inner_t)
 
 

time: 364 us -> 364 us (level)
  no operation moved by 1% of the time
where the time goes in v6:
time: 364 us; the launch traced here: 363 us
  blocking collectives  226 us (62%)
  matrix products  39.7 us (11%)
  Pallas kernels  34.2 us (9%)
  local copies, waits for them, and re-layouts  25.2 us (7%)
  starting transfers between devices  20.8 us (6%)
  waiting for transfers between devices  13.4 us (4%)
  other arithmetic  4.06 us (1%)
    all_gather x1, blocking collectives, on_device(): all_orbitals = lax.all_gather(orbitals, 'pcol', axis=0, tiled=True)  226 us
    pallas_call x1, Pallas kernels, build_blocks(): pl.pallas_call(tile_kernel, grid=(block_count // group,), in_specs=[pl.Bl...  34.2 us
    dot_general x1, matrix products, on_device(): jnp.einsum('gs,sqb->qgb', select, received_exchange, preferred_element_ty...  18.9 us
    convert_element_type x1, local copies, waits for them, and re-layouts, on_device(): slot_exchange = jnp.einsum('st,tqb->sqb', matches.astype(jnp.bfloat16), e...  17.9 us
    dot_general x1, matrix products, on_device(): jnp.einsum('st,tqb->sqb', matches.astype(jnp.bfloat16), exchange_ops, pre...  17.8 us
    all_to_all x1, waiting for transfers between devices, on_device(): lax.all_to_all(slot_exchange, ('prow', 'pcol'), 0, 0, tiled=True)  13.4 us
    all_to_all x1, starting transfers between devices, on_device(): received_small = lax.all_to_all(small, ('prow', 'pcol'), 0, 0, tiled=True)  10.6 us
    all_to_all x1, starting transfers between devices, on_device(): lax.all_to_all(slot_exchange, ('prow', 'pcol'), 0, 0, tiled=True)  10.2 us
  transfers between devices with their start and end apart: 2, of which 1 were waited for; matrix products, arithmetic and copies ran while one was open for 11% of the time, Pallas kernels for 0%

profile of v6, /device:TPU:23, one launch (start us, length us, event | category | flops | bytes accessed | tf_op | source)
XLA Modules:
  0.0 363.0 jit_solution(4552108644570486315)
XLA Ops:
  0.0 0.0 copy-start
  0.0 0.8 fusion.41
  0.8 0.8 fusion.40
  1.6 1.0 fusion.17
  2.6 0.0 copy-done
  2.6 0.6 fusion.42
  3.2 0.3 concatenate.6
  3.5 1.0 fusion.15
  4.6 0.9 copy.38
  5.5 0.9 select_reduce_fusion.2
  6.4 0.9 select_reduce_fusion
  7.3 0.3 convert_element_type.92
  7.6 0.3 convert_element_type.93
  7.9 0.3 convert_element_type.94
  8.2 2.3 concatenate.7
  10.5 10.6 %all-to-all-start = ((f32[128,2,640]{2,1,0:T(2,128)}), f32[128,2,640]{2,1,0:T(2,128)S(1)}, u32[]{:S(2)}, u32[]{:S(2)}) async-start(f32[128,2,640]{2,1,0:T(2,128)} %concatenate.7), calls=%async_computation | async-start | bytes 1310720 | tf_op jit(solution)/shard_map/all_to_all | solution.py:117
  21.1 17.8 %fusion.4 = bf16[256,128,256]{2,0,1:T(8,128)(2,1)} fusion(bf16[192,128,256]{2,1,0:T(8,128)(2,1)} %param.15, s32[192]{0:T(256)} %param.13), kind=kOutput, calls=%fused_computation.4 | convolution fusion | flops 3229663232 | bytes 29360896 | tf_op jit(solution)/shard_map/st,tqb->sqb/dot_general | solution.py:75
  38.9 17.9 %copy.43 = bf16[256,128,256]{2,1,0:T(8,128)(2,1)} copy(bf16[256,128,256]{2,0,1:T(8,128)(2,1)} %fusion.4) | data formatting | bytes 33554432 | tf_op jit(solution)/shard_map/convert_element_type | solution.py:80
  56.9 0.0 copy-start.3
  56.9 0.0 copy-start.2
  56.9 0.0 all-to-all-done
  56.9 10.2 %all-to-all-start.1 = ((bf16[256,128,256]{2,1,0:T(8,128)(2,1)}), bf16[256,128,256]{2,1,0:T(8,128)(2,1)}, u32[]{:S(2)}, u32[]{:S(2)}) async-start(bf16[256,128,256]{2,1,0:T(8,128)(2,1)} %copy.43), calls=%async_computation.1 | async-start | bytes 33554432 | tf_op jit(solution)/shard_map/all_to_all | solution.py:81
  67.1 0.0 copy-done.3
  67.1 225.5 %all-gather = bf16[16,4,512]{2,1,0:T(4,128)(2,1)S(1)} all-gather(bf16[1,4,512]{2,1,0:T(4,128)(2,1)S(1)} %bitcast.36), channel_id=1, replica_groups=mesh['prow'=8,'pcol'=16] {'pcol'}, dimensions={0}, use_global_device_ids=true | all-gather | bytes 69632 | tf_op jit(solution)/shard_map/all_gather | solution.py:119
  292.6 0.0 copy-done.2
  292.7 0.1 copy.45
  292.8 0.6 slice_bitcast_fusion.inner_t_ref
  293.4 0.9 convert_bitcast_fusion.basis_t_ref
  294.3 0.5 all_to_all.10
  294.7 0.1 slice_reduce_fusion
  294.9 0.3 fusion.23
  295.2 0.3 fusion.24
  295.5 1.1 fusion.13.weight_ref
  296.5 13.4 %all-to-all-done.1 = bf16[256,128,256]{2,1,0:T(8,128)(2,1)} async-done(((bf16[256,128,256]{2,1,0:T(8,128)(2,1)}), bf16[256,128,256]{2,1,0:T(8,128)(2,1)}, u32[]{:S(2)}, u32[]{:S(2)}) %all-to-all-start.1) | async-done | bytes 16777248 | tf_op jit(solution)/shard_map/all_to_all | solution.py:81
  309.9 0.0 copy-start.1
  309.9 18.9 %fusion.7.exchange_ref = f32[128,64,256]{2,1,0:T(8,128)} fusion(bf16[256,128,256]{2,1,0:T(8,128)(2,1)} %all-to-all-done.1, s32[256]{0:T(256)S(1)} %get-tuple-element.5), kind=kOutput, calls=%fused_computation.5 | convolution fusion | flops 1073758208 | bytes 25166848 | tf_op jit(solution)/shard_map/gs,sqb->qgb/dot_general | solution.py:143
  328.8 34.2 %shard_map.82 = bf16[64,256,256]{2,1,0:T(8,128)(2,1)} custom-call(f32[64,512]{1,0:T(8,128)} %fusion.13.weight_ref, f32[128,64,256]{2,1,0:T(8,128)} %fusion.7.exchange_ref, f32[256,512]{1,0:T(8,128)} %convert_bitcast_fusion.basis_t_ref, bf16[512,256]{1,0:T(8,128)(2,1)} %basis_ref.1, bf16[256,128]{1,0:T(8,128)(2,1)} %slice_bitcast_fusion.inner_t_ref), custom_call_target="tpu_custom_call" | custom-call | tf_op jit(solution)/shard_map/pallas_call | solution.py:41
  363.0 0.0 copy-done.1
  (7 shorter events, 0.1 us)
Async XLA Ops:
  0.0 2.6 copy-start
  10.5 46.4 %all-to-all-start = ((f32[128,2,640]{2,1,0:T(2,128)}), f32[128,2,640]{2,1,0:T(2,128)S(1)}, u32[]{:S(2)}, u32[]{:S(2)}) async-start(f32[128,2,640]{2,1,0:T(2,128)} %concatenate.7), calls=%async_computation | async-start | bytes 1310720 | tf_op jit(solution)/shard_map/all_to_all | solution.py:117
  56.9 10.2 %copy-start.3 = (bf16[4,512]{1,0:T(4,128)(2,1)S(1)}, bf16[4,512]{1,0:T(4,128)(2,1)}, u32[]{:S(2)}) copy-start(bf16[4,512]{1,0:T(4,128)(2,1)} %param.10) | copy-start | bytes 12292
  56.9 235.8 %copy-start.2 = (bf16[512,256]{1,0:T(8,128)(2,1)S(1)}, bf16[512,256]{1,0:T(8,128)(2,1)}, u32[]{:S(2)}) copy-start(bf16[512,256]{1,0:T(8,128)(2,1)} %basis_ref.1) | copy-start | bytes 786436
  56.9 253.1 %all-to-all-start.1 = ((bf16[256,128,256]{2,1,0:T(8,128)(2,1)}), bf16[256,128,256]{2,1,0:T(8,128)(2,1)}, u32[]{:S(2)}, u32[]{:S(2)}) async-start(bf16[256,128,256]{2,1,0:T(8,128)(2,1)} %copy.43), calls=%async_computation.1 | async-start | bytes 33554432 | tf_op jit(solution)/shard_map/all_to_all | solution.py:81
  309.9 53.1 %copy-start.1 = (f32[8,512]{1,0:T(8,128)S(1)}, f32[8,512]{1,0:T(8,128)}, u32[]{:S(2)}) copy-start(f32[8,512]{1,0:T(8,128)} %param.9) | copy-start | bytes 49156

commit v7 on v5

--- a/solution.py
+++ b/solution.py
@@ -2,6 +2,7 @@
 import jax.numpy as jnp
 from jax import lax
 from jax.experimental import pallas as pl
+from jax.experimental.pallas import tpu as pltpu
 from jax.sharding import PartitionSpec as P
 
 CAP = 2
@@ -15,37 +16,62 @@
     return high, low
 
 
-def tile_kernel(weight_ref, exchange_ref, basis_t_ref, basis_ref, inner_t_ref, out_ref):
+def local_kernel(weight_ref, basis_t_ref, basis_ref, out_ref):
     basis_t = basis_t_ref[...]
     basis = basis_ref[...]
-    inner_t = inner_t_ref[...]
     for j in range(out_ref.shape[0]):
         left = (basis_t * weight_ref[j : j + 1, :]).astype(jnp.bfloat16)
-        acc = jnp.dot(left, basis, preferred_element_type=jnp.float32)
+        out_ref[j] = jnp.dot(left, basis, preferred_element_type=jnp.float32)
+
+
+def exchange_kernel(local_ref, exchange_ref, inner_t_ref, out_ref, lhs_ref, rhs_ref):
+    inner_count = inner_t_ref.shape[1]
+    lhs_ref[:, :inner_count] = inner_t_ref[...]
+    lhs_ref[:, inner_count:] = inner_t_ref[...]
+    for j in range(out_ref.shape[0]):
         exchange_high, exchange_low = split_bf16(exchange_ref[:, j, :])
-        acc += jnp.dot(inner_t, exchange_high, preferred_element_type=jnp.float32)
-        acc += jnp.dot(inner_t, exchange_low, preferred_element_type=jnp.float32)
+        rhs_ref[:inner_count, :] = exchange_high
+        rhs_ref[inner_count:, :] = exchange_low
+        acc = local_ref[j] + jnp.dot(lhs_ref[...], rhs_ref[...], preferred_element_type=jnp.float32)
         out_ref[j] = acc.astype(out_ref.dtype)
 
 
-def build_blocks(weight_sum, exchange_sum, basis, group=8):
+def local_blocks(weight_sum, basis, group=8):
     block_count, point_count = weight_sum.shape
-    inner_count, _, spline_count = exchange_sum.shape
+    spline_count = basis.shape[1]
     basis_t = basis.T.astype(jnp.float32)
-    inner_t = basis[:inner_count].T
     return pl.pallas_call(
-        tile_kernel,
+        local_kernel,
         grid=(block_count // group,),
         in_specs=[
             pl.BlockSpec((group, point_count), lambda g: (g, 0)),
-            pl.BlockSpec((inner_count, group, spline_count), lambda g: (0, g, 0)),
             pl.BlockSpec((spline_count, point_count), lambda g: (0, 0)),
             pl.BlockSpec((point_count, spline_count), lambda g: (0, 0)),
+        ],
+        out_specs=pl.BlockSpec((group, spline_count, spline_count), lambda g: (g, 0, 0)),
+        out_shape=jax.ShapeDtypeStruct((block_count, spline_count, spline_count), jnp.float32),
+    )(weight_sum, basis_t, basis)
+
+
+def finish_blocks(local, exchange_sum, basis, group=8):
+    block_count, spline_count, _ = local.shape
+    inner_count = exchange_sum.shape[0]
+    inner_t = basis[:inner_count].T
+    return pl.pallas_call(
+        exchange_kernel,
+        grid=(block_count // group,),
+        in_specs=[
+            pl.BlockSpec((group, spline_count, spline_count), lambda g: (g, 0, 0)),
+            pl.BlockSpec((inner_count, group, spline_count), lambda g: (0, g, 0)),
             pl.BlockSpec((spline_count, inner_count), lambda g: (0, 0)),
         ],
         out_specs=pl.BlockSpec((group, spline_count, spline_count), lambda g: (g, 0, 0)),
         out_shape=jax.ShapeDtypeStruct((block_count, spline_count, spline_count), jnp.bfloat16),
-    )(weight_sum, exchange_sum, basis_t, basis, inner_t)
+        scratch_shapes=[
+            pltpu.VMEM((spline_count, 2 * inner_count), jnp.bfloat16),
+            pltpu.VMEM((2 * inner_count, spline_count), jnp.bfloat16),
+        ],
+    )(local, exchange_sum, inner_t)
 
 
 def on_device(basis, potentials, orbitals, chan_orbital, pair_list, slot_list, coefs, exchange_ops):
@@ -131,10 +157,11 @@
         jnp.bfloat16
     )
     weight_sum = jnp.dot(select, slot_weight, preferred_element_type=jnp.float32)
+    local = local_blocks(weight_sum, basis)
     exchange_sum = jnp.einsum(
         "gs,sqb->qgb", select, received_exchange, preferred_element_type=jnp.float32
     )
-    blocks = build_blocks(weight_sum, exchange_sum, basis)
+    blocks = finish_blocks(local, exchange_sum, basis)
     return blocks.reshape(RBLK, 1, BAND, 1, spline_count, spline_count)
 
 

time: 364 us -> 366 us (level); the launches traced: 363 us -> 360 us
  waiting for transfers between devices: 13.4 us -> 3.39 us
  Pallas kernels: 34.6 us -> 40.7 us
    all_to_all x1, waiting for transfers between devices: 13.4 us -> 3.39 us  [on_device(): lax.all_to_all(slot_exchange, ('prow', 'pcol'), 0, 0, tiled=True)]
    pallas_call x1 -> x2, Pallas kernels: 34.6 us -> 40.7 us  [the longest x1 30.7 us: finish_blocks(): pl.pallas_call(exchange_kernel, grid=(block_count // group,), in_specs=[p...]
  transfers between devices with their start and end apart: 2 -> 2, of which waited for: 1 -> 1; matrix products, arithmetic and copies ran while one was open for 11% -> 11% of each run, Pallas kernels for 0% -> 3%
where the time goes in v7:
time: 366 us; the launch traced here: 360 us
  blocking collectives  226 us (62%)
  Pallas kernels  40.7 us (11%)
  matrix products  39.7 us (11%)
  local copies, waits for them, and re-layouts  25.2 us (7%)
  starting transfers between devices  20.8 us (6%)
  other arithmetic  4.06 us (1%)
    all_gather x1, blocking collectives, on_device(): all_orbitals = lax.all_gather(orbitals, 'pcol', axis=0, tiled=True)  226 us
    pallas_call x1, Pallas kernels, finish_blocks(): pl.pallas_call(exchange_kernel, grid=(block_count // group,), in_specs=[p...  30.7 us
    dot_general x1, matrix products, on_device(): jnp.einsum('gs,sqb->qgb', select, received_exchange, preferred_element_ty...  18.9 us
    convert_element_type x1, local copies, waits for them, and re-layouts, on_device(): slot_exchange = jnp.einsum('st,tqb->sqb', matches.astype(jnp.bfloat16), e...  17.9 us
    dot_general x1, matrix products, on_device(): jnp.einsum('st,tqb->sqb', matches.astype(jnp.bfloat16), exchange_ops, pre...  17.8 us
    all_to_all x1, starting transfers between devices, on_device(): received_small = lax.all_to_all(small, ('prow', 'pcol'), 0, 0, tiled=True)  10.6 us
    all_to_all x1, starting transfers between devices, on_device(): lax.all_to_all(slot_exchange, ('prow', 'pcol'), 0, 0, tiled=True)  10.2 us
    pallas_call x1, Pallas kernels, local_blocks(): pl.pallas_call(local_kernel, grid=(block_count // group,), in_specs=[pl.B...  10 us
  transfers between devices with their start and end apart: 2, of which 1 were waited for; matrix products, arithmetic and copies ran while one was open for 11% of the time, Pallas kernels for 3%

profile of v7, /device:TPU:23, one launch (start us, length us, event | category | flops | bytes accessed | tf_op | source)
XLA Modules:
  0.0 359.5 jit_solution(14103317599774930308)
XLA Ops:
  0.0 0.0 copy-start
  0.0 0.8 fusion.40
  0.8 0.9 select_reduce_fusion.2
  1.8 0.9 select_reduce_fusion
  2.7 0.3 convert_element_type.92
  2.9 0.3 convert_element_type.93
  3.2 0.3 convert_element_type.94
  3.5 0.8 fusion.41
  4.2 1.0 fusion.17
  5.2 0.0 copy-done
  5.2 0.6 fusion.42
  5.9 0.3 concatenate.6
  6.2 1.0 fusion.15
  7.2 0.9 copy.38
  8.2 2.3 concatenate.7
  10.5 10.6 %all-to-all-start = ((f32[128,2,640]{2,1,0:T(2,128)}), f32[128,2,640]{2,1,0:T(2,128)S(1)}, u32[]{:S(2)}, u32[]{:S(2)}) async-start(f32[128,2,640]{2,1,0:T(2,128)} %concatenate.7), calls=%async_computation | async-start | bytes 1310720 | tf_op jit(solution)/shard_map/all_to_all | solution.py:134
  21.1 17.8 %fusion.4 = bf16[256,128,256]{2,0,1:T(8,128)(2,1)} fusion(bf16[192,128,256]{2,1,0:T(8,128)(2,1)} %param.15, s32[192]{0:T(256)} %param.13), kind=kOutput, calls=%fused_computation.4 | convolution fusion | flops 3229663232 | bytes 29360896 | tf_op jit(solution)/shard_map/st,tqb->sqb/dot_general | solution.py:92
  38.9 17.9 %copy.44 = bf16[256,128,256]{2,1,0:T(8,128)(2,1)} copy(bf16[256,128,256]{2,0,1:T(8,128)(2,1)} %fusion.4) | data formatting | bytes 33554432 | tf_op jit(solution)/shard_map/convert_element_type | solution.py:97
  56.9 0.0 copy-start.3
  56.9 0.0 copy-start.2
  56.9 0.0 all-to-all-done
  56.9 10.2 %all-to-all-start.1 = ((bf16[256,128,256]{2,1,0:T(8,128)(2,1)}), bf16[256,128,256]{2,1,0:T(8,128)(2,1)}, u32[]{:S(2)}, u32[]{:S(2)}) async-start(bf16[256,128,256]{2,1,0:T(8,128)(2,1)} %copy.44), calls=%async_computation.1 | async-start | bytes 33554432 | tf_op jit(solution)/shard_map/all_to_all | solution.py:98
  67.1 0.0 copy-done.3
  67.1 225.5 %all-gather = bf16[16,4,512]{2,1,0:T(4,128)(2,1)S(1)} all-gather(bf16[1,4,512]{2,1,0:T(4,128)(2,1)S(1)} %bitcast.36), channel_id=1, replica_groups=mesh['prow'=8,'pcol'=16] {'pcol'}, dimensions={0}, use_global_device_ids=true | all-gather | bytes 69632 | tf_op jit(solution)/shard_map/all_gather | solution.py:136
  292.6 0.0 copy-done.2
  292.7 0.1 copy.42
  292.8 0.6 slice_bitcast_fusion.inner_t_ref
  293.4 0.9 convert_bitcast_fusion.basis_t_ref
  294.3 0.5 all_to_all.10
  294.7 0.1 slice_reduce_fusion
  294.8 0.3 fusion.23
  295.2 0.3 fusion.24
  295.4 1.1 fusion.13.weight_ref
  296.5 10.0 %shard_map.82.local_ref = f32[64,256,256]{2,1,0:T(8,128)} custom-call(f32[64,512]{1,0:T(8,128)} %fusion.13.weight_ref, f32[256,512]{1,0:T(8,128)} %convert_bitcast_fusion.basis_t_ref, bf16[512,256]{1,0:T(8,128)(2,1)} %basis_ref.1), custom_call_target="tpu_custom_call" | custom-call | tf_op jit(solution)/shard_map/pallas_call | solution.py:43
  306.5 3.4 all-to-all-done.1
  309.9 0.0 copy-start.1
  309.9 18.9 %fusion.7.exchange_ref = f32[128,64,256]{2,1,0:T(8,128)} fusion(bf16[256,128,256]{2,1,0:T(8,128)(2,1)} %all-to-all-done.1, s32[256]{0:T(256)S(1)} %get-tuple-element.5), kind=kOutput, calls=%fused_computation.5 | convolution fusion | flops 1073758208 | bytes 25166848 | tf_op jit(solution)/shard_map/gs,sqb->qgb/dot_general | solution.py:161
  328.8 30.7 %shard_map.83 = bf16[64,256,256]{2,1,0:T(8,128)(2,1)} custom-call(f32[64,256,256]{2,1,0:T(8,128)} %shard_map.82.local_ref, f32[128,64,256]{2,1,0:T(8,128)} %fusion.7.exchange_ref, bf16[256,128]{1,0:T(8,128)(2,1)} %slice_bitcast_fusion.inner_t_ref), custom_call_target="tpu_custom_call" | custom-call | tf_op jit(solution)/shard_map/pallas_call | solution.py:60
  359.5 0.0 copy-done.1
  (7 shorter events, 0.1 us)
Async XLA Ops:
  0.0 5.2 %copy-start = (f32[8,512]{1,0:T(8,128)S(1)}, f32[8,512]{1,0:T(8,128)}, u32[]{:S(2)}) copy-start(f32[8,512]{1,0:T(8,128)} %param.9) | copy-start | bytes 49156
  10.5 46.4 %all-to-all-start = ((f32[128,2,640]{2,1,0:T(2,128)}), f32[128,2,640]{2,1,0:T(2,128)S(1)}, u32[]{:S(2)}, u32[]{:S(2)}) async-start(f32[128,2,640]{2,1,0:T(2,128)} %concatenate.7), calls=%async_computation | async-start | bytes 1310720 | tf_op jit(solution)/shard_map/all_to_all | solution.py:134
  56.9 10.2 %copy-start.3 = (bf16[4,512]{1,0:T(4,128)(2,1)S(1)}, bf16[4,512]{1,0:T(4,128)(2,1)}, u32[]{:S(2)}) copy-start(bf16[4,512]{1,0:T(4,128)(2,1)} %param.10) | copy-start | bytes 12292
  56.9 235.8 %copy-start.2 = (bf16[512,256]{1,0:T(8,128)(2,1)S(1)}, bf16[512,256]{1,0:T(8,128)(2,1)}, u32[]{:S(2)}) copy-start(bf16[512,256]{1,0:T(8,128)(2,1)} %basis_ref.1) | copy-start | bytes 786436
  56.9 253.1 %all-to-all-start.1 = ((bf16[256,128,256]{2,1,0:T(8,128)(2,1)}), bf16[256,128,256]{2,1,0:T(8,128)(2,1)}, u32[]{:S(2)}, u32[]{:S(2)}) async-start(bf16[256,128,256]{2,1,0:T(8,128)(2,1)} %copy.44), calls=%async_computation.1 | async-start | bytes 33554432 | tf_op jit(solution)/shard_map/all_to_all | solution.py:98
  309.9 49.6 %copy-start.1 = (f32[8,512]{1,0:T(8,128)S(1)}, f32[8,512]{1,0:T(8,128)}, u32[]{:S(2)}) copy-start(f32[8,512]{1,0:T(8,128)} %param.9) | copy-start | bytes 49156

commit v8 on v6

--- a/solution.py
+++ b/solution.py
@@ -25,7 +25,7 @@
     basis_t = basis_t_ref[...]
     for j in range(out_ref.shape[0]):
         lhs_ref[:, :point_count] = (basis_t * weight_ref[j : j + 1, :]).astype(jnp.bfloat16)
-        exchange_high, exchange_low = split_bf16(exchange_ref[:, j, :])
+        exchange_high, exchange_low = split_bf16(exchange_ref[j])
         rhs_ref[point_count : point_count + inner_count, :] = exchange_high
         rhs_ref[point_count + inner_count :, :] = exchange_low
         acc = jnp.dot(lhs_ref[...], rhs_ref[...], preferred_element_type=jnp.float32)
@@ -34,7 +34,7 @@
 
 def build_blocks(weight_sum, exchange_sum, basis, group=8):
     block_count, point_count = weight_sum.shape
-    inner_count, _, spline_count = exchange_sum.shape
+    inner_count, spline_count = exchange_sum.shape[1:]
     basis_t = basis.T.astype(jnp.float32)
     inner_t = basis[:inner_count].T
     depth = point_count + 2 * inner_count
@@ -43,7 +43,7 @@
         grid=(block_count // group,),
         in_specs=[
             pl.BlockSpec((group, point_count), lambda g: (g, 0)),
-            pl.BlockSpec((inner_count, group, spline_count), lambda g: (0, g, 0)),
+            pl.BlockSpec((group, inner_count, spline_count), lambda g: (g, 0, 0)),
             pl.BlockSpec((spline_count, point_count), lambda g: (0, 0)),
             pl.BlockSpec((point_count, spline_count), lambda g: (0, 0)),
             pl.BlockSpec((spline_count, inner_count), lambda g: (0, 0)),
@@ -141,7 +141,7 @@
     )
     weight_sum = jnp.dot(select, slot_weight, preferred_element_type=jnp.float32)
     exchange_sum = jnp.einsum(
-        "gs,sqb->qgb", select, received_exchange, preferred_element_type=jnp.float32
+        "gs,sqb->gqb", select, received_exchange, preferred_element_type=jnp.float32
     )
     blocks = build_blocks(weight_sum, exchange_sum, basis)
     return blocks.reshape(RBLK, 1, BAND, 1, spline_count, spline_count)

time: 364 us -> 349 us (0.959)
  Pallas kernels: 34.2 us -> 12.9 us
  local copies, waits for them, and re-layouts: 25.2 us -> 33.3 us
    pallas_call x1, Pallas kernels: 34.2 us -> 12.9 us  [build_blocks(): pl.pallas_call(tile_kernel, grid=(block_count // group,), in_specs=[pl.Bl...]
    dot_general x0 -> x1, local copies, waits for them, and re-layouts: none -> 8.08 us  [on_device(): jnp.einsum('gs,sqb->gqb', select, received_exchange, preferred_element_ty...]
where the time goes in v8:
time: 349 us; the launch traced here: 348 us
  blocking collectives  226 us (65%)
  matrix products  38.1 us (11%)
  local copies, waits for them, and re-layouts  33.3 us (10%)
  starting transfers between devices  20.8 us (6%)
  waiting for transfers between devices  13.4 us (4%)
  Pallas kernels  12.9 us (4%)
  other arithmetic  4.06 us (1%)
    all_gather x1, blocking collectives, on_device(): all_orbitals = lax.all_gather(orbitals, 'pcol', axis=0, tiled=True)  226 us
    convert_element_type x1, local copies, waits for them, and re-layouts, on_device(): slot_exchange = jnp.einsum('st,tqb->sqb', matches.astype(jnp.bfloat16), e...  17.9 us
    dot_general x1, matrix products, on_device(): jnp.einsum('st,tqb->sqb', matches.astype(jnp.bfloat16), exchange_ops, pre...  17.8 us
    dot_general x1, matrix products, on_device(): jnp.einsum('gs,sqb->gqb', select, received_exchange, preferred_element_ty...  17.4 us
    all_to_all x1, waiting for transfers between devices, on_device(): lax.all_to_all(slot_exchange, ('prow', 'pcol'), 0, 0, tiled=True)  13.4 us
    pallas_call x1, Pallas kernels, build_blocks(): pl.pallas_call(tile_kernel, grid=(block_count // group,), in_specs=[pl.Bl...  12.9 us
    all_to_all x1, starting transfers between devices, on_device(): received_small = lax.all_to_all(small, ('prow', 'pcol'), 0, 0, tiled=True)  10.6 us
    all_to_all x1, starting transfers between devices, on_device(): lax.all_to_all(slot_exchange, ('prow', 'pcol'), 0, 0, tiled=True)  10.2 us
  transfers between devices with their start and end apart: 2, of which 1 were waited for; matrix products, arithmetic and copies ran while one was open for 11% of the time, Pallas kernels for 0%

profile of v8, /device:TPU:23, one launch (start us, length us, event | category | flops | bytes accessed | tf_op | source)
XLA Modules:
  0.0 348.3 jit_solution(7372967359491531788)
XLA Ops:
  0.0 0.0 copy-start
  0.0 0.8 fusion.38
  0.8 0.8 fusion.37
  1.6 1.0 fusion.14
  2.6 0.0 copy-done
  2.6 0.6 fusion.39
  3.2 0.3 concatenate.6
  3.5 1.0 fusion.12
  4.6 0.9 copy.42
  5.5 0.9 select_reduce_fusion.2
  6.4 0.9 select_reduce_fusion
  7.3 0.3 convert_element_type.92
  7.6 0.3 convert_element_type.93
  7.9 0.3 convert_element_type.94
  8.2 2.3 concatenate.7
  10.5 10.6 %all-to-all-start = ((f32[128,2,640]{2,1,0:T(2,128)}), f32[128,2,640]{2,1,0:T(2,128)S(1)}, u32[]{:S(2)}, u32[]{:S(2)}) async-start(f32[128,2,640]{2,1,0:T(2,128)} %concatenate.7), calls=%async_computation | async-start | bytes 1310720 | tf_op jit(solution)/shard_map/all_to_all | solution.py:117
  21.1 17.8 %fusion.4 = bf16[256,128,256]{2,0,1:T(8,128)(2,1)} fusion(bf16[192,128,256]{2,1,0:T(8,128)(2,1)} %param.15, s32[192]{0:T(256)} %param.13), kind=kOutput, calls=%fused_computation.4 | convolution fusion | flops 3229663232 | bytes 29360896 | tf_op jit(solution)/shard_map/st,tqb->sqb/dot_general | solution.py:75
  38.9 17.9 %copy.47 = bf16[256,128,256]{2,1,0:T(8,128)(2,1)} copy(bf16[256,128,256]{2,0,1:T(8,128)(2,1)} %fusion.4) | data formatting | bytes 33554432 | tf_op jit(solution)/shard_map/convert_element_type | solution.py:80
  56.9 0.0 copy-start.3
  56.9 0.0 copy-start.2
  56.9 0.0 all-to-all-done
  56.9 10.2 %all-to-all-start.1 = ((bf16[256,128,256]{2,1,0:T(8,128)(2,1)}), bf16[256,128,256]{2,1,0:T(8,128)(2,1)}, u32[]{:S(2)}, u32[]{:S(2)}) async-start(bf16[256,128,256]{2,1,0:T(8,128)(2,1)} %copy.47), calls=%async_computation.1 | async-start | bytes 33554432 | tf_op jit(solution)/shard_map/all_to_all | solution.py:81
  67.1 0.0 copy-done.3
  67.1 225.5 %all-gather = bf16[16,4,512]{2,1,0:T(4,128)(2,1)S(1)} all-gather(bf16[1,4,512]{2,1,0:T(4,128)(2,1)S(1)} %bitcast.34), channel_id=1, replica_groups=mesh['prow'=8,'pcol'=16] {'pcol'}, dimensions={0}, use_global_device_ids=true | all-gather | bytes 69632 | tf_op jit(solution)/shard_map/all_gather | solution.py:119
  292.7 0.0 copy-done.2
  292.7 0.1 copy.49
  292.8 0.6 slice_bitcast_fusion.inner_t_ref
  293.4 0.9 convert_bitcast_fusion.basis_t_ref
  294.3 0.5 all_to_all.10
  294.8 0.1 slice_reduce_fusion
  294.9 0.3 fusion.20
  295.2 0.3 fusion.21
  295.5 1.1 fusion.10.weight_ref
  296.5 13.4 %all-to-all-done.1 = bf16[256,128,256]{2,1,0:T(8,128)(2,1)} async-done(((bf16[256,128,256]{2,1,0:T(8,128)(2,1)}), bf16[256,128,256]{2,1,0:T(8,128)(2,1)}, u32[]{:S(2)}, u32[]{:S(2)}) %all-to-all-start.1) | async-done | bytes 16777248 | tf_op jit(solution)/shard_map/all_to_all | solution.py:81
  310.0 0.0 copy-start.1
  310.0 17.4 %fusion = f32[64,128,256]{2,0,1:T(8,128)S(1)} fusion(bf16[256,128,256]{2,1,0:T(8,128)(2,1)} %all-to-all-done.1, s32[256]{0:T(256)S(1)} %get-tuple-element.5), kind=kOutput, calls=%fused_computation | convolution fusion | flops 1073758208 | bytes 25166848 | tf_op jit(solution)/shard_map/gs,sqb->gqb/dot_general | solution.py:143
  327.3 8.1 %copy.51.exchange_ref = f32[64,128,256]{2,1,0:T(8,128)} copy(f32[64,128,256]{2,0,1:T(8,128)S(1)} %fusion) | data formatting | bytes 16777216 | tf_op jit(solution)/shard_map/gs,sqb->gqb/dot_general | solution.py:143
  335.4 12.9 %shard_map.82 = bf16[64,256,256]{2,1,0:T(8,128)(2,1)} custom-call(f32[64,512]{1,0:T(8,128)} %fusion.10.weight_ref, f32[64,128,256]{2,1,0:T(8,128)} %copy.51.exchange_ref, f32[256,512]{1,0:T(8,128)} %convert_bitcast_fusion.basis_t_ref, bf16[512,256]{1,0:T(8,128)(2,1)} %basis_ref.1, bf16[256,128]{1,0:T(8,128)(2,1)} %slice_bitcast_fusion.inner_t_ref), custom_call_target="tpu_custom_call" | custom-call | tf_op jit(solution)/shard_map/pallas_call | solution.py:41
  348.3 0.0 copy-done.1
  (7 shorter events, 0.1 us)
Async XLA Ops:
  0.0 2.6 copy-start
  10.5 46.4 %all-to-all-start = ((f32[128,2,640]{2,1,0:T(2,128)}), f32[128,2,640]{2,1,0:T(2,128)S(1)}, u32[]{:S(2)}, u32[]{:S(2)}) async-start(f32[128,2,640]{2,1,0:T(2,128)} %concatenate.7), calls=%async_computation | async-start | bytes 1310720 | tf_op jit(solution)/shard_map/all_to_all | solution.py:117
  56.9 10.2 %copy-start.3 = (bf16[4,512]{1,0:T(4,128)(2,1)S(1)}, bf16[4,512]{1,0:T(4,128)(2,1)}, u32[]{:S(2)}) copy-start(bf16[4,512]{1,0:T(4,128)(2,1)} %param.10) | copy-start | bytes 12292
  56.9 235.8 %copy-start.2 = (bf16[512,256]{1,0:T(8,128)(2,1)S(1)}, bf16[512,256]{1,0:T(8,128)(2,1)}, u32[]{:S(2)}) copy-start(bf16[512,256]{1,0:T(8,128)(2,1)} %basis_ref.1) | copy-start | bytes 786436
  56.9 253.1 %all-to-all-start.1 = ((bf16[256,128,256]{2,1,0:T(8,128)(2,1)}), bf16[256,128,256]{2,1,0:T(8,128)(2,1)}, u32[]{:S(2)}, u32[]{:S(2)}) async-start(bf16[256,128,256]{2,1,0:T(8,128)(2,1)} %copy.47), calls=%async_computation.1 | async-start | bytes 33554432 | tf_op jit(solution)/shard_map/all_to_all | solution.py:81
  310.0 38.4 %copy-start.1 = (f32[8,512]{1,0:T(8,128)S(1)}, f32[8,512]{1,0:T(8,128)}, u32[]{:S(2)}) copy-start(f32[8,512]{1,0:T(8,128)} %param.9) | copy-start | bytes 49156

commit v9 on v8

--- a/solution.py
+++ b/solution.py
@@ -78,6 +78,19 @@
         exchange_ops,
         preferred_element_type=jnp.float32,
     ).astype(jnp.bfloat16)
+    orb_local = orbitals.shape[0]
+    all_orbitals = lax.dynamic_update_slice_in_dim(
+        jnp.zeros((orb_local * col_devs, orbitals.shape[1]), orbitals.dtype),
+        orbitals,
+        lax.axis_index("pcol") * orb_local,
+        0,
+    )
+    shift = 1
+    while shift < col_devs:
+        pairs = [(i, (i + shift) % col_devs) for i in range(col_devs)]
+        all_orbitals = all_orbitals + lax.ppermute(all_orbitals, "pcol", pairs)
+        shift *= 2
+    slot_exchange, all_orbitals = lax.optimization_barrier((slot_exchange, all_orbitals))
     received_exchange = lax.all_to_all(slot_exchange, ("prow", "pcol"), 0, 0, tiled=True)
 
     channels = jnp.arange(chan_count, dtype=jnp.int32)
@@ -116,7 +129,6 @@
     )
     received_small = lax.all_to_all(small, ("prow", "pcol"), 0, 0, tiled=True)
 
-    all_orbitals = lax.all_gather(orbitals, "pcol", axis=0, tiled=True)
     orb_ids = jnp.arange(all_orbitals.shape[0], dtype=jnp.int32)
     recv_first = received_small[:, point_count + 1].astype(jnp.int32)
     recv_second = received_small[:, point_count + 2].astype(jnp.int32)

time: 349 us -> 354 us (1.014); the launches traced: 348 us -> 349 us
  blocking collectives: 226 us -> 0 us
  waiting for transfers between devices: 13.4 us -> 229 us
  starting transfers between devices: 20.8 us -> 29 us
    all_gather x1 -> x0, blocking collectives: 226 us -> none  [on_device(): all_orbitals = lax.all_gather(orbitals, 'pcol', axis=0, tiled=True)]
    all_to_all x1, waiting for transfers between devices: 13.4 us -> 228 us  [on_device(): lax.all_to_all(slot_exchange, ('prow', 'pcol'), 0, 0, tiled=True)]
    optimization_barrier x0 -> x1, local copies, waits for them, and re-layouts: none -> 18 us  [on_device(): lax.optimization_barrier((slot_exchange, all_orbitals))]
    convert_element_type x1 -> x0, local copies, waits for them, and re-layouts: 17.9 us -> none  [on_device(): slot_exchange = jnp.einsum('st,tqb->sqb', matches.astype(jnp.bfloat16), e...]
    ppermute x0 -> x4, starting transfers between devices: none -> 6.58 us  [on_device(): all_orbitals = all_orbitals + lax.ppermute(all_orbitals, 'pcol', pairs)]
  transfers between devices with their start and end apart: 2 -> 6, of which waited for: 1 -> 2; matrix products, arithmetic and copies ran while one was open for 11% -> 14% of each run, Pallas kernels for 0% -> 0%
where the time goes in v9:
time: 354 us; the launch traced here: 349 us
  waiting for transfers between devices  229 us (65%)
  matrix products  38.4 us (11%)
  local copies, waits for them, and re-layouts  34 us (10%)
  starting transfers between devices  29 us (8%)
  Pallas kernels  12.9 us (4%)
  other arithmetic  4.82 us (1%)
    all_to_all x1, waiting for transfers between devices, on_device(): lax.all_to_all(slot_exchange, ('prow', 'pcol'), 0, 0, tiled=True)  228 us
    optimization_barrier x1, local copies, waits for them, and re-layouts, on_device(): lax.optimization_barrier((slot_exchange, all_orbitals))  18 us
    dot_general x1, matrix products, on_device(): jnp.einsum('st,tqb->sqb', matches.astype(jnp.bfloat16), exchange_ops, pre...  17.8 us
    dot_general x1, matrix products, on_device(): jnp.einsum('gs,sqb->gqb', select, received_exchange, preferred_element_ty...  17.6 us
    pallas_call x1, Pallas kernels, build_blocks(): pl.pallas_call(tile_kernel, grid=(block_count // group,), in_specs=[pl.Bl...  12.9 us
    all_to_all x1, starting transfers between devices, on_device(): received_small = lax.all_to_all(small, ('prow', 'pcol'), 0, 0, tiled=True)  11.3 us
    all_to_all x1, starting transfers between devices, on_device(): lax.all_to_all(slot_exchange, ('prow', 'pcol'), 0, 0, tiled=True)  11.1 us
    dot_general x1, local copies, waits for them, and re-layouts, on_device(): jnp.einsum('gs,sqb->gqb', select, received_exchange, preferred_element_ty...  8.08 us
  transfers between devices with their start and end apart: 6, of which 2 were waited for; matrix products, arithmetic and copies ran while one was open for 14% of the time, Pallas kernels for 0%

profile of v9, /device:TPU:23, one launch (start us, length us, event | category | flops | bytes accessed | tf_op | source)
XLA Modules:
  0.0 348.7 jit_solution(13169710541867478899)
XLA Ops:
  0.0 0.0 copy-start
  0.0 0.7 constant_dynamic-update-slice_fusion
  0.7 1.6 collective-permute-start
  2.4 0.8 fusion.37
  3.2 0.8 fusion.38
  4.0 1.0 fusion.14
  4.9 0.0 copy-done
  5.0 0.6 fusion.39
  5.6 1.0 fusion.12
  6.6 0.0 collective-permute-done
  6.7 0.7 add_dynamic-update-slice_fusion
  7.4 3.4 collective-permute-start.1
  10.7 0.9 select_reduce_fusion.2
  11.6 1.3 collective-permute-done.1
  13.0 1.1 collective-permute-start.2
  14.0 0.9 select_reduce_fusion
  14.9 0.3 convert_element_type.92
  15.2 0.3 convert_element_type.93
  15.5 0.3 convert_element_type.94
  15.7 0.3 concatenate.6
  16.1 0.9 copy.44
  17.0 2.3 concatenate.7
  19.3 11.3 %all-to-all-start = ((f32[128,2,640]{2,1,0:T(2,128)}), f32[128,2,640]{2,1,0:T(2,128)S(1)}, u32[]{:S(2)}, u32[]{:S(2)}) async-start(f32[128,2,640]{2,1,0:T(2,128)} %concatenate.7), calls=%async_computation | async-start | bytes 1310720 | tf_op jit(solution)/shard_map/all_to_all | solution.py:130
  30.6 0.0 collective-permute-done.2
  30.7 0.5 collective-permute-start.3
  31.2 17.8 %fusion.4 = bf16[256,128,256]{2,0,1:T(8,128)(2,1)} fusion(bf16[192,128,256]{2,1,0:T(8,128)(2,1)} %param.15, s32[192]{0:T(256)} %param.13), kind=kOutput, calls=%fused_computation.4 | convolution fusion | flops 3229663232 | bytes 29360896 | tf_op jit(solution)/shard_map/st,tqb->sqb/dot_general | solution.py:75
  49.0 0.0 collective-permute-done.3
  49.0 18.0 %copy.49 = bf16[256,128,256]{2,1,0:T(8,128)(2,1)} copy(bf16[256,128,256]{2,0,1:T(8,128)(2,1)} %fusion.4) | data formatting | bytes 33554432 | tf_op jit(solution)/shard_map/optimization_barrier | solution.py:93
  67.0 0.0 copy-start.2
  67.0 0.0 all-to-all-done
  67.0 11.1 %all-to-all-start.1 = ((bf16[256,128,256]{2,1,0:T(8,128)(2,1)}), bf16[256,128,256]{2,1,0:T(8,128)(2,1)}, u32[]{:S(2)}, u32[]{:S(2)}) async-start(bf16[256,128,256]{2,1,0:T(8,128)(2,1)} %copy.49), calls=%async_computation.1 | async-start | bytes 33554432 | tf_op jit(solution)/shard_map/all_to_all | solution.py:94
  78.1 0.0 copy-done.2
  78.1 0.1 copy.51
  78.2 0.6 slice_bitcast_fusion.inner_t_ref
  78.9 0.9 convert_bitcast_fusion.basis_t_ref
  79.7 0.5 all_to_all.10
  80.2 0.1 slice_reduce_fusion
  80.3 0.3 fusion.20
  80.6 0.3 fusion.21
  80.9 1.1 fusion.10.weight_ref
  81.9 228.1 %all-to-all-done.1 = bf16[256,128,256]{2,1,0:T(8,128)(2,1)} async-done(((bf16[256,128,256]{2,1,0:T(8,128)(2,1)}), bf16[256,128,256]{2,1,0:T(8,128)(2,1)}, u32[]{:S(2)}, u32[]{:S(2)}) %all-to-all-start.1) | async-done | bytes 16777248 | tf_op jit(solution)/shard_map/all_to_all | solution.py:94
  310.0 0.0 copy-start.1
  310.0 17.6 %fusion = f32[64,128,256]{2,0,1:T(8,128)S(1)} fusion(bf16[256,128,256]{2,1,0:T(8,128)(2,1)} %all-to-all-done.1, s32[256]{0:T(256)S(1)} %get-tuple-element.9), kind=kOutput, calls=%fused_computation | convolution fusion | flops 1073758208 | bytes 25166848 | tf_op jit(solution)/shard_map/gs,sqb->gqb/dot_general | solution.py:155
  327.7 8.1 %copy.53.exchange_ref = f32[64,128,256]{2,1,0:T(8,128)} copy(f32[64,128,256]{2,0,1:T(8,128)S(1)} %fusion) | data formatting | bytes 16777216 | tf_op jit(solution)/shard_map/gs,sqb->gqb/dot_general | solution.py:155
  335.7 12.9 %shard_map.82 = bf16[64,256,256]{2,1,0:T(8,128)(2,1)} custom-call(f32[64,512]{1,0:T(8,128)} %fusion.10.weight_ref, f32[64,128,256]{2,1,0:T(8,128)} %copy.53.exchange_ref, f32[256,512]{1,0:T(8,128)} %convert_bitcast_fusion.basis_t_ref, bf16[512,256]{1,0:T(8,128)(2,1)} %basis_ref.1, bf16[256,128]{1,0:T(8,128)(2,1)} %slice_bitcast_fusion.inner_t_ref), custom_call_target="tpu_custom_call" | custom-call | tf_op jit(solution)/shard_map/pallas_call | solution.py:41
  348.6 0.0 copy-done.1
  (10 shorter events, 0.1 us)
Async XLA Ops:
  0.0 5.0 %copy-start = (f32[8,512]{1,0:T(8,128)S(1)}, f32[8,512]{1,0:T(8,128)}, u32[]{:S(2)}) copy-start(f32[8,512]{1,0:T(8,128)} %param.9) | copy-start | bytes 49156
  0.7 5.9 %collective-permute-start = (bf16[64,512]{1,0:T(8,128)(2,1)S(1)}, bf16[64,512]{1,0:T(8,128)(2,1)S(1)}, u32[]{:S(2)}, u32[]{:S(2)}) collective-permute-start(bf16[64,512]{1,0:T(8,128)(2,1)S(1)} %constant_dynamic-update-slice_fusion), channel_id=1, source_target_pairs={{0,1},{1,2},{2,3},{3,4},{4,5},{5,6},{6,7},{7,8},{8,9},{9,10},{10,1... | collective-permute-start | bytes 196616 | tf_op jit(solution)/shard_map/ppermute | solution.py:91
  7.4 5.6 %collective-permute-start.1 = (bf16[64,512]{1,0:T(8,128)(2,1)S(1)}, bf16[64,512]{1,0:T(8,128)(2,1)S(1)}, u32[]{:S(2)}, u32[]{:S(2)}) collective-permute-start(bf16[64,512]{1,0:T(8,128)(2,1)S(1)} %add_dynamic-update-slice_fusion), channel_id=1, source_target_pairs={{0,2},{1,3},{2,4},{3,5},{4,6},{5,7},{6,8},{7,9},{8,10},{9,11},{10,... | collective-permute-start | bytes 196616 | tf_op jit(solution)/shard_map/ppermute | solution.py:91
  13.0 17.7 %collective-permute-start.2 = (bf16[64,512]{1,0:T(8,128)(2,1)S(1)}, bf16[64,512]{1,0:T(8,128)(2,1)S(1)}, u32[]{:S(2)}, u32[]{:S(2)}) collective-permute-start(bf16[64,512]{1,0:T(8,128)(2,1)S(1)} %add.59), channel_id=1, source_target_pairs={{0,4},{1,5},{2,6},{3,7},{4,8},{5,9},{6,10},{7,11},{8,12},{9,13},{1... | collective-permute-start | bytes 196616 | tf_op jit(solution)/shard_map/ppermute | solution.py:91
  19.3 47.7 %all-to-all-start = ((f32[128,2,640]{2,1,0:T(2,128)}), f32[128,2,640]{2,1,0:T(2,128)S(1)}, u32[]{:S(2)}, u32[]{:S(2)}) async-start(f32[128,2,640]{2,1,0:T(2,128)} %concatenate.7), calls=%async_computation | async-start | bytes 1310720 | tf_op jit(solution)/shard_map/all_to_all | solution.py:130
  30.7 18.3 %collective-permute-start.3 = (bf16[64,512]{1,0:T(8,128)(2,1)S(1)}, bf16[64,512]{1,0:T(8,128)(2,1)S(1)}, u32[]{:S(2)}, u32[]{:S(2)}) collective-permute-start(bf16[64,512]{1,0:T(8,128)(2,1)S(1)} %add.60), channel_id=1, source_target_pairs={{0,8},{1,9},{2,10},{3,11},{4,12},{5,13},{6,14},{7,15},{8,0},{9,1},... | collective-permute-start | bytes 196616 | tf_op jit(solution)/shard_map/ppermute | solution.py:91
  67.0 11.1 %copy-start.2 = (bf16[512,256]{1,0:T(8,128)(2,1)S(1)}, bf16[512,256]{1,0:T(8,128)(2,1)}, u32[]{:S(2)}) copy-start(bf16[512,256]{1,0:T(8,128)(2,1)} %basis_ref.1) | copy-start | bytes 786436
  67.0 243.1 %all-to-all-start.1 = ((bf16[256,128,256]{2,1,0:T(8,128)(2,1)}), bf16[256,128,256]{2,1,0:T(8,128)(2,1)}, u32[]{:S(2)}, u32[]{:S(2)}) async-start(bf16[256,128,256]{2,1,0:T(8,128)(2,1)} %copy.49), calls=%async_computation.1 | async-start | bytes 33554432 | tf_op jit(solution)/shard_map/all_to_all | solution.py:94
  310.0 38.6 %copy-start.1 = (f32[8,512]{1,0:T(8,128)S(1)}, f32[8,512]{1,0:T(8,128)}, u32[]{:S(2)}) copy-start(f32[8,512]{1,0:T(8,128)} %param.9) | copy-start | bytes 49156

commit v10 on v9

--- a/solution.py
+++ b/solution.py
@@ -79,17 +79,21 @@
         preferred_element_type=jnp.float32,
     ).astype(jnp.bfloat16)
     orb_local = orbitals.shape[0]
+    col_index = lax.axis_index("pcol")
     all_orbitals = lax.dynamic_update_slice_in_dim(
         jnp.zeros((orb_local * col_devs, orbitals.shape[1]), orbitals.dtype),
         orbitals,
-        lax.axis_index("pcol") * orb_local,
+        col_index * orb_local,
         0,
     )
-    shift = 1
-    while shift < col_devs:
+    for shift in range(1, col_devs):
         pairs = [(i, (i + shift) % col_devs) for i in range(col_devs)]
-        all_orbitals = all_orbitals + lax.ppermute(all_orbitals, "pcol", pairs)
-        shift *= 2
+        all_orbitals = lax.dynamic_update_slice_in_dim(
+            all_orbitals,
+            lax.ppermute(orbitals, "pcol", pairs),
+            ((col_index - shift) % col_devs) * orb_local,
+            0,
+        )
     slot_exchange, all_orbitals = lax.optimization_barrier((slot_exchange, all_orbitals))
     received_exchange = lax.all_to_all(slot_exchange, ("prow", "pcol"), 0, 0, tiled=True)
 

time: 354 us -> 377 us (1.065)
  starting transfers between devices: 29 us -> 53.4 us
    ppermute x4 -> x15, starting transfers between devices: 6.58 us -> 27.1 us  [on_device(): lax.ppermute(orbitals, 'pcol', pairs)]
    all_to_all x1, starting transfers between devices: 11.1 us -> 15.3 us  [on_device(): lax.all_to_all(slot_exchange, ('prow', 'pcol'), 0, 0, tiled=True)]
  transfers between devices with their start and end apart: 6 -> 17, of which waited for: 2 -> 2; matrix products, arithmetic and copies ran while one was open for 14% -> 13% of each run, Pallas kernels for 0% -> 0%
where the time goes in v10:
time: 377 us; the launch traced here: 372 us
  waiting for transfers between devices  229 us (61%)
  starting transfers between devices  53.4 us (14%)
  matrix products  38.4 us (10%)
  local copies, waits for them, and re-layouts  33.5 us (9%)
  Pallas kernels  12.9 us (3%)
  other arithmetic  4.06 us (1%)
    all_to_all x1, waiting for transfers between devices, on_device(): lax.all_to_all(slot_exchange, ('prow', 'pcol'), 0, 0, tiled=True)  228 us
    ppermute x15, starting transfers between devices, on_device(): lax.ppermute(orbitals, 'pcol', pairs)  27.1 us
    optimization_barrier x1, local copies, waits for them, and re-layouts, on_device(): lax.optimization_barrier((slot_exchange, all_orbitals))  18 us
    dot_general x1, matrix products, on_device(): jnp.einsum('st,tqb->sqb', matches.astype(jnp.bfloat16), exchange_ops, pre...  17.8 us
    dot_general x1, matrix products, on_device(): jnp.einsum('gs,sqb->gqb', select, received_exchange, preferred_element_ty...  17.6 us
    all_to_all x1, starting transfers between devices, on_device(): lax.all_to_all(slot_exchange, ('prow', 'pcol'), 0, 0, tiled=True)  15.3 us
    pallas_call x1, Pallas kernels, build_blocks(): pl.pallas_call(tile_kernel, grid=(block_count // group,), in_specs=[pl.Bl...  12.9 us
    all_to_all x1, starting transfers between devices, on_device(): received_small = lax.all_to_all(small, ('prow', 'pcol'), 0, 0, tiled=True)  11 us
  transfers between devices with their start and end apart: 17, of which 2 were waited for; matrix products, arithmetic and copies ran while one was open for 13% of the time, Pallas kernels for 0%

profile of v10, /device:TPU:23, one launch (start us, length us, event | category | flops | bytes accessed | tf_op | source)
XLA Modules:
  0.0 371.7 jit_solution(9636323936396059604)
XLA Ops:
  0.0 1.6 collective-permute-start
  1.6 3.3 collective-permute-start.1
  4.9 1.4 collective-permute-start.2
  6.4 1.7 collective-permute-start.4
  8.1 0.8 fusion.37
  8.9 0.9 select_reduce_fusion.2
  9.8 0.9 select_reduce_fusion
  10.7 0.3 convert_element_type.92
  11.0 0.3 convert_element_type.93
  11.3 0.3 convert_element_type.94
  11.6 0.8 fusion.38
  12.3 1.0 fusion.14
  13.3 0.6 fusion.39
  14.0 0.3 concatenate.6
  14.3 1.0 fusion.12
  15.3 0.9 copy.44
  16.2 2.3 concatenate.7
  18.6 11.0 %all-to-all-start = ((f32[128,2,640]{2,1,0:T(2,128)}), f32[128,2,640]{2,1,0:T(2,128)S(1)}, u32[]{:S(2)}, u32[]{:S(2)}) async-start(f32[128,2,640]{2,1,0:T(2,128)} %concatenate.7), calls=%async_computation | async-start | bytes 1310720 | tf_op jit(solution)/shard_map/all_to_all | solution.py:134
  29.8 0.0 copy-start.3
  29.8 17.8 %fusion.4 = bf16[256,128,256]{2,0,1:T(8,128)(2,1)} fusion(bf16[192,128,256]{2,1,0:T(8,128)(2,1)} %param.15, s32[192]{0:T(256)} %param.13), kind=kOutput, calls=%fused_computation.4 | convolution fusion | flops 3229663232 | bytes 29360896 | tf_op jit(solution)/shard_map/st,tqb->sqb/dot_general | solution.py:75
  47.9 0.0 collective-permute-done
  47.9 4.0 %collective-permute-start.5 = (bf16[4,512]{1,0:T(4,128)(2,1)S(1)}, bf16[4,512]{1,0:T(4,128)(2,1)S(1)}, u32[]{:S(2)}, u32[]{:S(2)}) collective-permute-start(bf16[4,512]{1,0:T(4,128)(2,1)S(1)} %copy-done.3), channel_id=1, source_target_pairs={{0,6},{1,7},{2,8},{3,9},{4,10},{5,11},{6,12},{7,13},{8,14},{9,15},... | collective-permute-start | bytes 12296 | tf_op jit(solution)/shard_map/ppermute | solution.py:93
  51.8 1.5 collective-permute-start.6
  53.3 0.0 collective-permute-done.2
  53.3 1.6 collective-permute-start.7
  54.9 0.0 collective-permute-done.3
  54.9 1.7 collective-permute-start.8
  56.6 2.0 collective-permute-start.9
  58.6 4.2 %collective-permute-start.10 = (bf16[4,512]{1,0:T(4,128)(2,1)S(1)}, bf16[4,512]{1,0:T(4,128)(2,1)S(1)}, u32[]{:S(2)}, u32[]{:S(2)}) collective-permute-start(bf16[4,512]{1,0:T(4,128)(2,1)S(1)} %copy-done.3), channel_id=1, source_target_pairs={{0,11},{1,12},{2,13},{3,14},{4,15},{5,0},{6,1},{7,2},{8,3},{9,4},{... | collective-permute-start | bytes 12296 | tf_op jit(solution)/shard_map/ppermute | solution.py:93
  62.8 0.1 collective-permute-start.11
  62.9 0.1 collective-permute-start.12
  63.0 2.1 collective-permute-start.13
  65.1 1.9 collective-permute-start.14
  67.2 0.6 collective-permute-done.14
  67.8 18.0 %copy.49 = bf16[256,128,256]{2,1,0:T(8,128)(2,1)} copy(bf16[256,128,256]{2,0,1:T(8,128)(2,1)} %fusion.4) | data formatting | bytes 33554432 | tf_op jit(solution)/shard_map/optimization_barrier | solution.py:97
  85.8 15.3 %all-to-all-start.1 = ((bf16[256,128,256]{2,1,0:T(8,128)(2,1)}), bf16[256,128,256]{2,1,0:T(8,128)(2,1)}, u32[]{:S(2)}, u32[]{:S(2)}) async-start(bf16[256,128,256]{2,1,0:T(8,128)(2,1)} %copy.49), calls=%async_computation.1 | async-start | bytes 33554432 | tf_op jit(solution)/shard_map/all_to_all | solution.py:98
  101.1 0.1 copy.51
  101.3 0.6 slice_bitcast_fusion.inner_t_ref
  101.9 0.9 convert_bitcast_fusion.basis_t_ref
  102.8 0.5 all_to_all.10
  103.2 0.1 slice_reduce_fusion
  103.3 0.3 fusion.20
  103.7 0.3 fusion.21
  103.9 1.1 fusion.10.weight_ref
  105.0 228.1 %all-to-all-done.1 = bf16[256,128,256]{2,1,0:T(8,128)(2,1)} async-done(((bf16[256,128,256]{2,1,0:T(8,128)(2,1)}), bf16[256,128,256]{2,1,0:T(8,128)(2,1)}, u32[]{:S(2)}, u32[]{:S(2)}) %all-to-all-start.1) | async-done | bytes 16777248 | tf_op jit(solution)/shard_map/all_to_all | solution.py:98
  333.1 17.6 %fusion = f32[64,128,256]{2,0,1:T(8,128)S(1)} fusion(bf16[256,128,256]{2,1,0:T(8,128)(2,1)} %all-to-all-done.1, s32[256]{0:T(256)S(1)} %get-tuple-element.9), kind=kOutput, calls=%fused_computation | convolution fusion | flops 1073758208 | bytes 25166848 | tf_op jit(solution)/shard_map/gs,sqb->gqb/dot_general | solution.py:159
  350.7 8.1 %copy.53.exchange_ref = f32[64,128,256]{2,1,0:T(8,128)} copy(f32[64,128,256]{2,0,1:T(8,128)S(1)} %fusion) | data formatting | bytes 16777216 | tf_op jit(solution)/shard_map/gs,sqb->gqb/dot_general | solution.py:159
  358.8 12.9 %shard_map.82 = bf16[64,256,256]{2,1,0:T(8,128)(2,1)} custom-call(f32[64,512]{1,0:T(8,128)} %fusion.10.weight_ref, f32[64,128,256]{2,1,0:T(8,128)} %copy.53.exchange_ref, f32[256,512]{1,0:T(8,128)} %convert_bitcast_fusion.basis_t_ref, bf16[512,256]{1,0:T(8,128)(2,1)} %basis_ref.1, bf16[256,128]{1,0:T(8,128)(2,1)} %slice_bitcast_fusion.inner_t_ref), custom_call_target="tpu_custom_call" | custom-call | tf_op jit(solution)/shard_map/pallas_call | solution.py:41
  (43 shorter events, 0.3 us)
Async XLA Ops:
  0.0 13.3 %copy-start = (f32[8,512]{1,0:T(8,128)S(1)}, f32[8,512]{1,0:T(8,128)}, u32[]{:S(2)}) copy-start(f32[8,512]{1,0:T(8,128)} %param.9) | copy-start | bytes 49156
  0.0 47.9 %collective-permute-start = (bf16[4,512]{1,0:T(4,128)(2,1)}, bf16[4,512]{1,0:T(4,128)(2,1)S(1)}, u32[]{:S(2)}, u32[]{:S(2)}) collective-permute-start(bf16[4,512]{1,0:T(4,128)(2,1)} %param.10), channel_id=1, source_target_pairs={{0,1},{1,2},{2,3},{3,4},{4,5},{5,6},{6,7},{7,8},{8,9},{9,10},{10,1... | collective-permute-start | bytes 12296 | tf_op jit(solution)/shard_map/ppermute | solution.py:93
  1.6 50.2 %collective-permute-start.1 = (bf16[4,512]{1,0:T(4,128)(2,1)}, bf16[4,512]{1,0:T(4,128)(2,1)S(1)}, u32[]{:S(2)}, u32[]{:S(2)}) collective-permute-start(bf16[4,512]{1,0:T(4,128)(2,1)} %param.10), channel_id=1, source_target_pairs={{0,2},{1,3},{2,4},{3,5},{4,6},{5,7},{6,8},{7,9},{8,10},{9,11},{10,... | collective-permute-start | bytes 12296 | tf_op jit(solution)/shard_map/ppermute | solution.py:93
  4.9 48.4 %collective-permute-start.2 = (bf16[4,512]{1,0:T(4,128)(2,1)}, bf16[4,512]{1,0:T(4,128)(2,1)S(1)}, u32[]{:S(2)}, u32[]{:S(2)}) collective-permute-start(bf16[4,512]{1,0:T(4,128)(2,1)} %param.10), channel_id=1, source_target_pairs={{0,3},{1,4},{2,5},{3,6},{4,7},{5,8},{6,9},{7,10},{8,11},{9,12},{10... | collective-permute-start | bytes 12296 | tf_op jit(solution)/shard_map/ppermute | solution.py:93
  6.4 48.5 %collective-permute-start.3 = (bf16[4,512]{1,0:T(4,128)(2,1)}, bf16[4,512]{1,0:T(4,128)(2,1)S(1)}, u32[]{:S(2)}, u32[]{:S(2)}) collective-permute-start(bf16[4,512]{1,0:T(4,128)(2,1)} %param.10), channel_id=1, source_target_pairs={{0,4},{1,5},{2,6},{3,7},{4,8},{5,9},{6,10},{7,11},{8,12},{9,13},{1... | collective-permute-start | bytes 12296 | tf_op jit(solution)/shard_map/ppermute | solution.py:93
  6.4 50.2 %collective-permute-start.4 = (bf16[4,512]{1,0:T(4,128)(2,1)}, bf16[4,512]{1,0:T(4,128)(2,1)S(1)}, u32[]{:S(2)}, u32[]{:S(2)}) collective-permute-start(bf16[4,512]{1,0:T(4,128)(2,1)} %param.10), channel_id=1, source_target_pairs={{0,5},{1,6},{2,7},{3,8},{4,9},{5,10},{6,11},{7,12},{8,13},{9,14},{... | collective-permute-start | bytes 12296 | tf_op jit(solution)/shard_map/ppermute | solution.py:93
  18.6 67.2 %all-to-all-start = ((f32[128,2,640]{2,1,0:T(2,128)}), f32[128,2,640]{2,1,0:T(2,128)S(1)}, u32[]{:S(2)}, u32[]{:S(2)}) async-start(f32[128,2,640]{2,1,0:T(2,128)} %concatenate.7), calls=%async_computation | async-start | bytes 1310720 | tf_op jit(solution)/shard_map/all_to_all | solution.py:134
  29.8 17.9 %copy-start.3 = (bf16[4,512]{1,0:T(4,128)(2,1)S(1)}, bf16[4,512]{1,0:T(4,128)(2,1)}, u32[]{:S(2)}) copy-start(bf16[4,512]{1,0:T(4,128)(2,1)} %param.10) | copy-start | bytes 12292
  47.9 10.7 %collective-permute-start.5 = (bf16[4,512]{1,0:T(4,128)(2,1)S(1)}, bf16[4,512]{1,0:T(4,128)(2,1)S(1)}, u32[]{:S(2)}, u32[]{:S(2)}) collective-permute-start(bf16[4,512]{1,0:T(4,128)(2,1)S(1)} %copy-done.3), channel_id=1, source_target_pairs={{0,6},{1,7},{2,8},{3,9},{4,10},{5,11},{6,12},{7,13},{8,14},{9,15},... | collective-permute-start | bytes 12296 | tf_op jit(solution)/shard_map/ppermute | solution.py:93
  51.8 10.9 %collective-permute-start.6 = (bf16[4,512]{1,0:T(4,128)(2,1)S(1)}, bf16[4,512]{1,0:T(4,128)(2,1)S(1)}, u32[]{:S(2)}, u32[]{:S(2)}) collective-permute-start(bf16[4,512]{1,0:T(4,128)(2,1)S(1)} %copy-done.3), channel_id=1, source_target_pairs={{0,7},{1,8},{2,9},{3,10},{4,11},{5,12},{6,13},{7,14},{8,15},{9,0},... | collective-permute-start | bytes 12296 | tf_op jit(solution)/shard_map/ppermute | solution.py:93
  53.3 9.6 %collective-permute-start.7 = (bf16[4,512]{1,0:T(4,128)(2,1)S(1)}, bf16[4,512]{1,0:T(4,128)(2,1)S(1)}, u32[]{:S(2)}, u32[]{:S(2)}) collective-permute-start(bf16[4,512]{1,0:T(4,128)(2,1)S(1)} %copy-done.3), channel_id=1, source_target_pairs={{0,8},{1,9},{2,10},{3,11},{4,12},{5,13},{6,14},{7,15},{8,0},{9,1},... | collective-permute-start | bytes 12296 | tf_op jit(solution)/shard_map/ppermute | solution.py:93
  54.9 8.1 %collective-permute-start.8 = (bf16[4,512]{1,0:T(4,128)(2,1)S(1)}, bf16[4,512]{1,0:T(4,128)(2,1)S(1)}, u32[]{:S(2)}, u32[]{:S(2)}) collective-permute-start(bf16[4,512]{1,0:T(4,128)(2,1)S(1)} %copy-done.3), channel_id=1, source_target_pairs={{0,9},{1,10},{2,11},{3,12},{4,13},{5,14},{6,15},{7,0},{8,1},{9,2},... | collective-permute-start | bytes 12296 | tf_op jit(solution)/shard_map/ppermute | solution.py:93
  56.6 8.5 %collective-permute-start.9 = (bf16[4,512]{1,0:T(4,128)(2,1)S(1)}, bf16[4,512]{1,0:T(4,128)(2,1)S(1)}, u32[]{:S(2)}, u32[]{:S(2)}) collective-permute-start(bf16[4,512]{1,0:T(4,128)(2,1)S(1)} %copy-done.3), channel_id=1, source_target_pairs={{0,10},{1,11},{2,12},{3,13},{4,14},{5,15},{6,0},{7,1},{8,2},{9,3},... | collective-permute-start | bytes 12296 | tf_op jit(solution)/shard_map/ppermute | solution.py:93
  58.6 8.4 %collective-permute-start.10 = (bf16[4,512]{1,0:T(4,128)(2,1)S(1)}, bf16[4,512]{1,0:T(4,128)(2,1)S(1)}, u32[]{:S(2)}, u32[]{:S(2)}) collective-permute-start(bf16[4,512]{1,0:T(4,128)(2,1)S(1)} %copy-done.3), channel_id=1, source_target_pairs={{0,11},{1,12},{2,13},{3,14},{4,15},{5,0},{6,1},{7,2},{8,3},{9,4},{... | collective-permute-start | bytes 12296 | tf_op jit(solution)/shard_map/ppermute | solution.py:93
  62.8 4.3 %collective-permute-start.11 = (bf16[4,512]{1,0:T(4,128)(2,1)S(1)}, bf16[4,512]{1,0:T(4,128)(2,1)S(1)}, u32[]{:S(2)}, u32[]{:S(2)}) collective-permute-start(bf16[4,512]{1,0:T(4,128)(2,1)S(1)} %copy-done.3), channel_id=1, source_target_pairs={{0,12},{1,13},{2,14},{3,15},{4,0},{5,1},{6,2},{7,3},{8,4},{9,5},{1... | collective-permute-start | bytes 12296 | tf_op jit(solution)/shard_map/ppermute | solution.py:93
  62.9 4.2 %collective-permute-start.12 = (bf16[4,512]{1,0:T(4,128)(2,1)S(1)}, bf16[4,512]{1,0:T(4,128)(2,1)S(1)}, u32[]{:S(2)}, u32[]{:S(2)}) collective-permute-start(bf16[4,512]{1,0:T(4,128)(2,1)S(1)} %copy-done.3), channel_id=1, source_target_pairs={{0,13},{1,14},{2,15},{3,0},{4,1},{5,2},{6,3},{7,4},{8,5},{9,6},{10... | collective-permute-start | bytes 12296 | tf_op jit(solution)/shard_map/ppermute | solution.py:93
  63.0 4.1 %collective-permute-start.13 = (bf16[4,512]{1,0:T(4,128)(2,1)S(1)}, bf16[4,512]{1,0:T(4,128)(2,1)S(1)}, u32[]{:S(2)}, u32[]{:S(2)}) collective-permute-start(bf16[4,512]{1,0:T(4,128)(2,1)S(1)} %copy-done.3), channel_id=1, source_target_pairs={{0,14},{1,15},{2,0},{3,1},{4,2},{5,3},{6,4},{7,5},{8,6},{9,7},{10,... | collective-permute-start | bytes 12296 | tf_op jit(solution)/shard_map/ppermute | solution.py:93
  65.1 2.7 collective-permute-start.14
  85.8 15.4 %copy-start.2 = (bf16[512,256]{1,0:T(8,128)(2,1)S(1)}, bf16[512,256]{1,0:T(8,128)(2,1)}, u32[]{:S(2)}) copy-start(bf16[512,256]{1,0:T(8,128)(2,1)} %basis_ref.1) | copy-start | bytes 786436
  85.8 247.3 %all-to-all-start.1 = ((bf16[256,128,256]{2,1,0:T(8,128)(2,1)}), bf16[256,128,256]{2,1,0:T(8,128)(2,1)}, u32[]{:S(2)}, u32[]{:S(2)}) async-start(bf16[256,128,256]{2,1,0:T(8,128)(2,1)} %copy.49), calls=%async_computation.1 | async-start | bytes 33554432 | tf_op jit(solution)/shard_map/all_to_all | solution.py:98
  333.1 38.6 %copy-start.1 = (f32[8,512]{1,0:T(8,128)S(1)}, f32[8,512]{1,0:T(8,128)}, u32[]{:S(2)}) copy-start(f32[8,512]{1,0:T(8,128)} %param.9) | copy-start | bytes 49156

commit v11 on v8

--- a/solution.py
+++ b/solution.py
@@ -18,16 +18,12 @@
 
 def tile_kernel(weight_ref, exchange_ref, basis_t_ref, basis_ref, inner_t_ref, out_ref, lhs_ref, rhs_ref):
     point_count = basis_ref.shape[0]
-    inner_count = inner_t_ref.shape[1]
-    lhs_ref[:, point_count : point_count + inner_count] = inner_t_ref[...]
-    lhs_ref[:, point_count + inner_count :] = inner_t_ref[...]
+    lhs_ref[:, point_count:] = inner_t_ref[...]
     rhs_ref[:point_count, :] = basis_ref[...]
     basis_t = basis_t_ref[...]
     for j in range(out_ref.shape[0]):
         lhs_ref[:, :point_count] = (basis_t * weight_ref[j : j + 1, :]).astype(jnp.bfloat16)
-        exchange_high, exchange_low = split_bf16(exchange_ref[j])
-        rhs_ref[point_count : point_count + inner_count, :] = exchange_high
-        rhs_ref[point_count + inner_count :, :] = exchange_low
+        rhs_ref[point_count:, :] = exchange_ref[j]
         acc = jnp.dot(lhs_ref[...], rhs_ref[...], preferred_element_type=jnp.float32)
         out_ref[j] = acc.astype(out_ref.dtype)
 
@@ -37,7 +33,7 @@
     inner_count, spline_count = exchange_sum.shape[1:]
     basis_t = basis.T.astype(jnp.float32)
     inner_t = basis[:inner_count].T
-    depth = point_count + 2 * inner_count
+    depth = point_count + inner_count
     return pl.pallas_call(
         tile_kernel,
         grid=(block_count // group,),
@@ -142,7 +138,7 @@
     weight_sum = jnp.dot(select, slot_weight, preferred_element_type=jnp.float32)
     exchange_sum = jnp.einsum(
         "gs,sqb->gqb", select, received_exchange, preferred_element_type=jnp.float32
-    )
+    ).astype(jnp.bfloat16)
     blocks = build_blocks(weight_sum, exchange_sum, basis)
     return blocks.reshape(RBLK, 1, BAND, 1, spline_count, spline_count)
 

time: 349 us -> 343 us (0.983)
  local copies, waits for them, and re-layouts: 33.3 us -> 29.8 us
where the time goes in v11:
time: 343 us; the launch traced here: 342 us
  blocking collectives  226 us (66%)
  matrix products  36.4 us (11%)
  local copies, waits for them, and re-layouts  29.8 us (9%)
  starting transfers between devices  20.8 us (6%)
  waiting for transfers between devices  13.4 us (4%)
  Pallas kernels  11.8 us (3%)
  other arithmetic  4.06 us (1%)
    all_gather x1, blocking collectives, on_device(): all_orbitals = lax.all_gather(orbitals, 'pcol', axis=0, tiled=True)  226 us
    convert_element_type x1, local copies, waits for them, and re-layouts, on_device(): slot_exchange = jnp.einsum('st,tqb->sqb', matches.astype(jnp.bfloat16), e...  17.9 us
    dot_general x1, matrix products, on_device(): jnp.einsum('st,tqb->sqb', matches.astype(jnp.bfloat16), exchange_ops, pre...  17.8 us
    dot_general x1, matrix products, on_device(): jnp.einsum('gs,sqb->gqb', select, received_exchange, preferred_element_ty...  15.6 us
    all_to_all x1, waiting for transfers between devices, on_device(): lax.all_to_all(slot_exchange, ('prow', 'pcol'), 0, 0, tiled=True)  13.4 us
    pallas_call x1, Pallas kernels, build_blocks(): pl.pallas_call(tile_kernel, grid=(block_count // group,), in_specs=[pl.Bl...  11.8 us
    all_to_all x1, starting transfers between devices, on_device(): received_small = lax.all_to_all(small, ('prow', 'pcol'), 0, 0, tiled=True)  10.6 us
    all_to_all x1, starting transfers between devices, on_device(): lax.all_to_all(slot_exchange, ('prow', 'pcol'), 0, 0, tiled=True)  10.2 us
  transfers between devices with their start and end apart: 2, of which 1 were waited for; matrix products, arithmetic and copies ran while one was open for 11% of the time, Pallas kernels for 0%

profile of v11, /device:TPU:23, one launch (start us, length us, event | category | flops | bytes accessed | tf_op | source)
XLA Modules:
  0.0 342.0 jit_solution(3777622769898479800)
XLA Ops:
  0.0 0.0 copy-start
  0.0 0.8 fusion.38
  0.8 0.8 fusion.37
  1.6 1.0 fusion.14
  2.6 0.0 copy-done
  2.6 0.6 fusion.39
  3.2 0.3 concatenate.6
  3.5 1.0 fusion.12
  4.6 0.9 copy.42
  5.5 0.9 select_reduce_fusion.2
  6.4 0.9 select_reduce_fusion
  7.3 0.3 convert_element_type.96
  7.6 0.3 convert_element_type.97
  7.9 0.3 convert_element_type.98
  8.2 2.3 concatenate.7
  10.5 10.6 %all-to-all-start = ((f32[128,2,640]{2,1,0:T(2,128)}), f32[128,2,640]{2,1,0:T(2,128)S(1)}, u32[]{:S(2)}, u32[]{:S(2)}) async-start(f32[128,2,640]{2,1,0:T(2,128)} %concatenate.7), calls=%async_computation | async-start | bytes 1310720 | tf_op jit(solution)/shard_map/all_to_all | solution.py:113
  21.1 17.8 %fusion.4 = bf16[256,128,256]{2,0,1:T(8,128)(2,1)} fusion(bf16[192,128,256]{2,1,0:T(8,128)(2,1)} %param.15, s32[192]{0:T(256)} %param.13), kind=kOutput, calls=%fused_computation.4 | convolution fusion | flops 3229663232 | bytes 29360896 | tf_op jit(solution)/shard_map/st,tqb->sqb/dot_general | solution.py:71
  38.9 17.9 %copy.47 = bf16[256,128,256]{2,1,0:T(8,128)(2,1)} copy(bf16[256,128,256]{2,0,1:T(8,128)(2,1)} %fusion.4) | data formatting | bytes 33554432 | tf_op jit(solution)/shard_map/convert_element_type | solution.py:76
  56.9 0.0 copy-start.3
  56.9 0.0 copy-start.2
  56.9 0.0 all-to-all-done
  56.9 10.2 %all-to-all-start.1 = ((bf16[256,128,256]{2,1,0:T(8,128)(2,1)}), bf16[256,128,256]{2,1,0:T(8,128)(2,1)}, u32[]{:S(2)}, u32[]{:S(2)}) async-start(bf16[256,128,256]{2,1,0:T(8,128)(2,1)} %copy.47), calls=%async_computation.1 | async-start | bytes 33554432 | tf_op jit(solution)/shard_map/all_to_all | solution.py:77
  67.1 0.0 copy-done.3
  67.1 225.5 %all-gather = bf16[16,4,512]{2,1,0:T(4,128)(2,1)S(1)} all-gather(bf16[1,4,512]{2,1,0:T(4,128)(2,1)S(1)} %bitcast.34), channel_id=1, replica_groups=mesh['prow'=8,'pcol'=16] {'pcol'}, dimensions={0}, use_global_device_ids=true | all-gather | bytes 69632 | tf_op jit(solution)/shard_map/all_gather | solution.py:115
  292.7 0.0 copy-done.2
  292.7 0.1 copy.50
  292.8 0.6 slice_bitcast_fusion.inner_t_ref
  293.4 0.9 convert_bitcast_fusion.basis_t_ref
  294.3 0.5 all_to_all.10
  294.8 0.1 slice_reduce_fusion
  294.9 0.3 fusion.20
  295.2 0.3 fusion.21
  295.5 0.0 copy-start.1
  295.5 1.1 fusion.10.weight_ref
  296.5 13.4 %all-to-all-done.1 = bf16[256,128,256]{2,1,0:T(8,128)(2,1)} async-done(((bf16[256,128,256]{2,1,0:T(8,128)(2,1)}), bf16[256,128,256]{2,1,0:T(8,128)(2,1)}, u32[]{:S(2)}, u32[]{:S(2)}) %all-to-all-start.1) | async-done | bytes 16777248 | tf_op jit(solution)/shard_map/all_to_all | solution.py:77
  310.0 15.6 %fusion = bf16[64,128,256]{2,0,1:T(8,128)(2,1)S(1)} fusion(bf16[256,128,256]{2,1,0:T(8,128)(2,1)} %all-to-all-done.1, s32[256]{0:T(256)S(1)} %get-tuple-element.5), kind=kOutput, calls=%fused_computation | convolution fusion | flops 1073758208 | bytes 20972544 | tf_op jit(solution)/shard_map/gs,sqb->gqb/dot_general | solution.py:139
  325.6 4.6 %copy.67.exchange_ref = bf16[64,128,256]{2,1,0:T(8,128)(2,1)} copy(bf16[64,128,256]{2,0,1:T(8,128)(2,1)S(1)} %fusion) | data formatting | bytes 8388608 | tf_op jit(solution)/shard_map/gs,sqb->gqb/dot_general | solution.py:139
  330.2 11.8 %shard_map.82 = bf16[64,256,256]{2,1,0:T(8,128)(2,1)} custom-call(f32[64,512]{1,0:T(8,128)} %fusion.10.weight_ref, bf16[64,128,256]{2,1,0:T(8,128)(2,1)} %copy.67.exchange_ref, f32[256,512]{1,0:T(8,128)} %convert_bitcast_fusion.basis_t_ref, bf16[512,256]{1,0:T(8,128)(2,1)} %basis_ref.1, bf16[256,128]{1,0:T(8,128)(2,1)} %slice_bitcast_fusion.inner_t_ref), custom_call_target="tpu_custom_call" | custom-call | tf_op jit(solution)/shard_map/pallas_call | solution.py:37
  342.0 0.0 copy-done.1
  (7 shorter events, 0.1 us)
Async XLA Ops:
  0.0 2.6 copy-start
  10.5 46.4 %all-to-all-start = ((f32[128,2,640]{2,1,0:T(2,128)}), f32[128,2,640]{2,1,0:T(2,128)S(1)}, u32[]{:S(2)}, u32[]{:S(2)}) async-start(f32[128,2,640]{2,1,0:T(2,128)} %concatenate.7), calls=%async_computation | async-start | bytes 1310720 | tf_op jit(solution)/shard_map/all_to_all | solution.py:113
  56.9 10.2 %copy-start.3 = (bf16[4,512]{1,0:T(4,128)(2,1)S(1)}, bf16[4,512]{1,0:T(4,128)(2,1)}, u32[]{:S(2)}) copy-start(bf16[4,512]{1,0:T(4,128)(2,1)} %param.10) | copy-start | bytes 12292
  56.9 235.8 %copy-start.2 = (bf16[512,256]{1,0:T(8,128)(2,1)S(1)}, bf16[512,256]{1,0:T(8,128)(2,1)}, u32[]{:S(2)}) copy-start(bf16[512,256]{1,0:T(8,128)(2,1)} %basis_ref.1) | copy-start | bytes 786436
  56.9 253.1 %all-to-all-start.1 = ((bf16[256,128,256]{2,1,0:T(8,128)(2,1)}), bf16[256,128,256]{2,1,0:T(8,128)(2,1)}, u32[]{:S(2)}, u32[]{:S(2)}) async-start(bf16[256,128,256]{2,1,0:T(8,128)(2,1)} %copy.47), calls=%async_computation.1 | async-start | bytes 33554432 | tf_op jit(solution)/shard_map/all_to_all | solution.py:77
  295.5 46.5 %copy-start.1 = (f32[8,512]{1,0:T(8,128)S(1)}, f32[8,512]{1,0:T(8,128)}, u32[]{:S(2)}) copy-start(f32[8,512]{1,0:T(8,128)} %param.9) | copy-start | bytes 49156

commit v12 on v11

--- a/solution.py
+++ b/solution.py
@@ -28,7 +28,7 @@
         out_ref[j] = acc.astype(out_ref.dtype)
 
 
-def build_blocks(weight_sum, exchange_sum, basis, group=8):
+def build_blocks(weight_sum, exchange_sum, basis, group=16):
     block_count, point_count = weight_sum.shape
     inner_count, spline_count = exchange_sum.shape[1:]
     basis_t = basis.T.astype(jnp.float32)

time: 343 us -> 341 us (level)
  transfers between devices with their start and end apart: 2 -> 2, of which waited for: 1 -> 1; matrix products, arithmetic and copies ran while one was open for 11% -> 12% of each run, Pallas kernels for 0% -> 0%
where the time goes in v12:
time: 341 us; the launch traced here: 340 us
  blocking collectives  226 us (66%)
  matrix products  36.4 us (11%)
  local copies, waits for them, and re-layouts  29.8 us (9%)
  starting transfers between devices  20.8 us (6%)
  waiting for transfers between devices  13.4 us (4%)
  Pallas kernels  10.3 us (3%)
  other arithmetic  4.06 us (1%)
    all_gather x1, blocking collectives, on_device(): all_orbitals = lax.all_gather(orbitals, 'pcol', axis=0, tiled=True)  226 us
    convert_element_type x1, local copies, waits for them, and re-layouts, on_device(): slot_exchange = jnp.einsum('st,tqb->sqb', matches.astype(jnp.bfloat16), e...  17.9 us
    dot_general x1, matrix products, on_device(): jnp.einsum('st,tqb->sqb', matches.astype(jnp.bfloat16), exchange_ops, pre...  17.8 us
    dot_general x1, matrix products, on_device(): jnp.einsum('gs,sqb->gqb', select, received_exchange, preferred_element_ty...  15.6 us
    all_to_all x1, waiting for transfers between devices, on_device(): lax.all_to_all(slot_exchange, ('prow', 'pcol'), 0, 0, tiled=True)  13.4 us
    all_to_all x1, starting transfers between devices, on_device(): received_small = lax.all_to_all(small, ('prow', 'pcol'), 0, 0, tiled=True)  10.6 us
    pallas_call x1, Pallas kernels, build_blocks(): pl.pallas_call(tile_kernel, grid=(block_count // group,), in_specs=[pl.Bl...  10.3 us
    all_to_all x1, starting transfers between devices, on_device(): lax.all_to_all(slot_exchange, ('prow', 'pcol'), 0, 0, tiled=True)  10.2 us
  transfers between devices with their start and end apart: 2, of which 1 were waited for; matrix products, arithmetic and copies ran while one was open for 12% of the time, Pallas kernels for 0%

profile of v12, /device:TPU:23, one launch (start us, length us, event | category | flops | bytes accessed | tf_op | source)
XLA Modules:
  0.0 340.5 jit_solution(2102637439632291803)
XLA Ops:
  0.0 0.0 copy-start
  0.0 0.8 fusion.38
  0.8 0.8 fusion.37
  1.6 1.0 fusion.14
  2.6 0.0 copy-done
  2.6 0.6 fusion.39
  3.2 0.3 concatenate.6
  3.5 1.0 fusion.12
  4.6 0.9 copy.42
  5.5 0.9 select_reduce_fusion.2
  6.4 0.9 select_reduce_fusion
  7.3 0.3 convert_element_type.96
  7.6 0.3 convert_element_type.97
  7.9 0.3 convert_element_type.98
  8.2 2.3 concatenate.7
  10.5 10.6 %all-to-all-start = ((f32[128,2,640]{2,1,0:T(2,128)}), f32[128,2,640]{2,1,0:T(2,128)S(1)}, u32[]{:S(2)}, u32[]{:S(2)}) async-start(f32[128,2,640]{2,1,0:T(2,128)} %concatenate.7), calls=%async_computation | async-start | bytes 1310720 | tf_op jit(solution)/shard_map/all_to_all | solution.py:113
  21.1 17.8 %fusion.4 = bf16[256,128,256]{2,0,1:T(8,128)(2,1)} fusion(bf16[192,128,256]{2,1,0:T(8,128)(2,1)} %param.15, s32[192]{0:T(256)} %param.13), kind=kOutput, calls=%fused_computation.4 | convolution fusion | flops 3229663232 | bytes 29360896 | tf_op jit(solution)/shard_map/st,tqb->sqb/dot_general | solution.py:71
  38.9 17.9 %copy.47 = bf16[256,128,256]{2,1,0:T(8,128)(2,1)} copy(bf16[256,128,256]{2,0,1:T(8,128)(2,1)} %fusion.4) | data formatting | bytes 33554432 | tf_op jit(solution)/shard_map/convert_element_type | solution.py:76
  56.9 0.0 copy-start.3
  56.9 0.0 copy-start.2
  56.9 0.0 all-to-all-done
  56.9 10.2 %all-to-all-start.1 = ((bf16[256,128,256]{2,1,0:T(8,128)(2,1)}), bf16[256,128,256]{2,1,0:T(8,128)(2,1)}, u32[]{:S(2)}, u32[]{:S(2)}) async-start(bf16[256,128,256]{2,1,0:T(8,128)(2,1)} %copy.47), calls=%async_computation.1 | async-start | bytes 33554432 | tf_op jit(solution)/shard_map/all_to_all | solution.py:77
  67.1 0.0 copy-done.3
  67.1 225.5 %all-gather = bf16[16,4,512]{2,1,0:T(4,128)(2,1)S(1)} all-gather(bf16[1,4,512]{2,1,0:T(4,128)(2,1)S(1)} %bitcast.34), channel_id=1, replica_groups=mesh['prow'=8,'pcol'=16] {'pcol'}, dimensions={0}, use_global_device_ids=true | all-gather | bytes 69632 | tf_op jit(solution)/shard_map/all_gather | solution.py:115
  292.7 0.0 copy-done.2
  292.7 0.1 copy.50
  292.8 0.6 slice_bitcast_fusion.inner_t_ref
  293.4 0.9 convert_bitcast_fusion.basis_t_ref
  294.3 0.5 all_to_all.10
  294.8 0.1 slice_reduce_fusion
  294.9 0.3 fusion.20
  295.2 0.3 fusion.21
  295.5 0.0 copy-start.1
  295.5 1.1 fusion.10.weight_ref
  296.5 13.4 %all-to-all-done.1 = bf16[256,128,256]{2,1,0:T(8,128)(2,1)} async-done(((bf16[256,128,256]{2,1,0:T(8,128)(2,1)}), bf16[256,128,256]{2,1,0:T(8,128)(2,1)}, u32[]{:S(2)}, u32[]{:S(2)}) %all-to-all-start.1) | async-done | bytes 16777248 | tf_op jit(solution)/shard_map/all_to_all | solution.py:77
  310.0 15.6 %fusion = bf16[64,128,256]{2,0,1:T(8,128)(2,1)S(1)} fusion(bf16[256,128,256]{2,1,0:T(8,128)(2,1)} %all-to-all-done.1, s32[256]{0:T(256)S(1)} %get-tuple-element.5), kind=kOutput, calls=%fused_computation | convolution fusion | flops 1073758208 | bytes 20972544 | tf_op jit(solution)/shard_map/gs,sqb->gqb/dot_general | solution.py:139
  325.6 4.6 %copy.67.exchange_ref = bf16[64,128,256]{2,1,0:T(8,128)(2,1)} copy(bf16[64,128,256]{2,0,1:T(8,128)(2,1)S(1)} %fusion) | data formatting | bytes 8388608 | tf_op jit(solution)/shard_map/gs,sqb->gqb/dot_general | solution.py:139
  330.2 10.3 %shard_map.82 = bf16[64,256,256]{2,1,0:T(8,128)(2,1)} custom-call(f32[64,512]{1,0:T(8,128)} %fusion.10.weight_ref, bf16[64,128,256]{2,1,0:T(8,128)(2,1)} %copy.67.exchange_ref, f32[256,512]{1,0:T(8,128)} %convert_bitcast_fusion.basis_t_ref, bf16[512,256]{1,0:T(8,128)(2,1)} %basis_ref.1, bf16[256,128]{1,0:T(8,128)(2,1)} %slice_bitcast_fusion.inner_t_ref), custom_call_target="tpu_custom_call" | custom-call | tf_op jit(solution)/shard_map/pallas_call | solution.py:37
  340.5 0.0 copy-done.1
  (7 shorter events, 0.1 us)
Async XLA Ops:
  0.0 2.6 copy-start
  10.5 46.4 %all-to-all-start = ((f32[128,2,640]{2,1,0:T(2,128)}), f32[128,2,640]{2,1,0:T(2,128)S(1)}, u32[]{:S(2)}, u32[]{:S(2)}) async-start(f32[128,2,640]{2,1,0:T(2,128)} %concatenate.7), calls=%async_computation | async-start | bytes 1310720 | tf_op jit(solution)/shard_map/all_to_all | solution.py:113
  56.9 10.2 %copy-start.3 = (bf16[4,512]{1,0:T(4,128)(2,1)S(1)}, bf16[4,512]{1,0:T(4,128)(2,1)}, u32[]{:S(2)}) copy-start(bf16[4,512]{1,0:T(4,128)(2,1)} %param.10) | copy-start | bytes 12292
  56.9 235.8 %copy-start.2 = (bf16[512,256]{1,0:T(8,128)(2,1)S(1)}, bf16[512,256]{1,0:T(8,128)(2,1)}, u32[]{:S(2)}) copy-start(bf16[512,256]{1,0:T(8,128)(2,1)} %basis_ref.1) | copy-start | bytes 786436
  56.9 253.1 %all-to-all-start.1 = ((bf16[256,128,256]{2,1,0:T(8,128)(2,1)}), bf16[256,128,256]{2,1,0:T(8,128)(2,1)}, u32[]{:S(2)}, u32[]{:S(2)}) async-start(bf16[256,128,256]{2,1,0:T(8,128)(2,1)} %copy.47), calls=%async_computation.1 | async-start | bytes 33554432 | tf_op jit(solution)/shard_map/all_to_all | solution.py:77
  295.5 45.0 %copy-start.1 = (f32[8,512]{1,0:T(8,128)S(1)}, f32[8,512]{1,0:T(8,128)}, u32[]{:S(2)}) copy-start(f32[8,512]{1,0:T(8,128)} %param.9) | copy-start | bytes 49156

commit v13 on v12

--- a/solution.py
+++ b/solution.py
@@ -28,7 +28,7 @@
         out_ref[j] = acc.astype(out_ref.dtype)
 
 
-def build_blocks(weight_sum, exchange_sum, basis, group=16):
+def build_blocks(weight_sum, exchange_sum, basis, group=32):
     block_count, point_count = weight_sum.shape
     inner_count, spline_count = exchange_sum.shape[1:]
     basis_t = basis.T.astype(jnp.float32)

time: 341 us -> 342 us (level)
  transfers between devices with their start and end apart: 2 -> 2, of which waited for: 1 -> 1; matrix products, arithmetic and copies ran while one was open for 12% -> 11% of each run, Pallas kernels for 0% -> 0%
where the time goes in v13:
time: 342 us; the launch traced here: 341 us
  blocking collectives  226 us (66%)
  matrix products  36.4 us (11%)
  local copies, waits for them, and re-layouts  29.8 us (9%)
  starting transfers between devices  20.8 us (6%)
  waiting for transfers between devices  13.4 us (4%)
  Pallas kernels  10.7 us (3%)
  other arithmetic  4.06 us (1%)
    all_gather x1, blocking collectives, on_device(): all_orbitals = lax.all_gather(orbitals, 'pcol', axis=0, tiled=True)  226 us
    convert_element_type x1, local copies, waits for them, and re-layouts, on_device(): slot_exchange = jnp.einsum('st,tqb->sqb', matches.astype(jnp.bfloat16), e...  17.9 us
    dot_general x1, matrix products, on_device(): jnp.einsum('st,tqb->sqb', matches.astype(jnp.bfloat16), exchange_ops, pre...  17.8 us
    dot_general x1, matrix products, on_device(): jnp.einsum('gs,sqb->gqb', select, received_exchange, preferred_element_ty...  15.6 us
    all_to_all x1, waiting for transfers between devices, on_device(): lax.all_to_all(slot_exchange, ('prow', 'pcol'), 0, 0, tiled=True)  13.4 us
    pallas_call x1, Pallas kernels, build_blocks(): pl.pallas_call(tile_kernel, grid=(block_count // group,), in_specs=[pl.Bl...  10.7 us
    all_to_all x1, starting transfers between devices, on_device(): received_small = lax.all_to_all(small, ('prow', 'pcol'), 0, 0, tiled=True)  10.6 us
    all_to_all x1, starting transfers between devices, on_device(): lax.all_to_all(slot_exchange, ('prow', 'pcol'), 0, 0, tiled=True)  10.2 us
  transfers between devices with their start and end apart: 2, of which 1 were waited for; matrix products, arithmetic and copies ran while one was open for 11% of the time, Pallas kernels for 0%

profile of v13, /device:TPU:23, one launch (start us, length us, event | category | flops | bytes accessed | tf_op | source)
XLA Modules:
  0.0 340.9 jit_solution(15267204582296534113)
XLA Ops:
  0.0 0.0 copy-start
  0.0 0.8 fusion.38
  0.8 0.8 fusion.37
  1.6 1.0 fusion.14
  2.6 0.0 copy-done
  2.6 0.6 fusion.39
  3.2 0.3 concatenate.6
  3.5 1.0 fusion.12
  4.6 0.9 copy.42
  5.5 0.9 select_reduce_fusion.2
  6.4 0.9 select_reduce_fusion
  7.3 0.3 convert_element_type.96
  7.6 0.3 convert_element_type.97
  7.9 0.3 convert_element_type.98
  8.2 2.3 concatenate.7
  10.5 10.6 %all-to-all-start = ((f32[128,2,640]{2,1,0:T(2,128)}), f32[128,2,640]{2,1,0:T(2,128)S(1)}, u32[]{:S(2)}, u32[]{:S(2)}) async-start(f32[128,2,640]{2,1,0:T(2,128)} %concatenate.7), calls=%async_computation | async-start | bytes 1310720 | tf_op jit(solution)/shard_map/all_to_all | solution.py:113
  21.1 17.8 %fusion.4 = bf16[256,128,256]{2,0,1:T(8,128)(2,1)} fusion(bf16[192,128,256]{2,1,0:T(8,128)(2,1)} %param.15, s32[192]{0:T(256)} %param.13), kind=kOutput, calls=%fused_computation.4 | convolution fusion | flops 3229663232 | bytes 29360896 | tf_op jit(solution)/shard_map/st,tqb->sqb/dot_general | solution.py:71
  38.9 17.9 %copy.47 = bf16[256,128,256]{2,1,0:T(8,128)(2,1)} copy(bf16[256,128,256]{2,0,1:T(8,128)(2,1)} %fusion.4) | data formatting | bytes 33554432 | tf_op jit(solution)/shard_map/convert_element_type | solution.py:76
  56.9 0.0 copy-start.3
  56.9 0.0 copy-start.2
  56.9 0.0 all-to-all-done
  56.9 10.2 %all-to-all-start.1 = ((bf16[256,128,256]{2,1,0:T(8,128)(2,1)}), bf16[256,128,256]{2,1,0:T(8,128)(2,1)}, u32[]{:S(2)}, u32[]{:S(2)}) async-start(bf16[256,128,256]{2,1,0:T(8,128)(2,1)} %copy.47), calls=%async_computation.1 | async-start | bytes 33554432 | tf_op jit(solution)/shard_map/all_to_all | solution.py:77
  67.1 0.0 copy-done.3
  67.1 225.5 %all-gather = bf16[16,4,512]{2,1,0:T(4,128)(2,1)S(1)} all-gather(bf16[1,4,512]{2,1,0:T(4,128)(2,1)S(1)} %bitcast.34), channel_id=1, replica_groups=mesh['prow'=8,'pcol'=16] {'pcol'}, dimensions={0}, use_global_device_ids=true | all-gather | bytes 69632 | tf_op jit(solution)/shard_map/all_gather | solution.py:115
  292.7 0.0 copy-done.2
  292.7 0.1 copy.50
  292.8 0.6 slice_bitcast_fusion.inner_t_ref
  293.4 0.9 convert_bitcast_fusion.basis_t_ref
  294.3 0.5 all_to_all.10
  294.8 0.1 slice_reduce_fusion
  294.9 0.3 fusion.20
  295.2 0.3 fusion.21
  295.5 0.0 copy-start.1
  295.5 1.1 fusion.10.weight_ref
  296.5 13.4 %all-to-all-done.1 = bf16[256,128,256]{2,1,0:T(8,128)(2,1)} async-done(((bf16[256,128,256]{2,1,0:T(8,128)(2,1)}), bf16[256,128,256]{2,1,0:T(8,128)(2,1)}, u32[]{:S(2)}, u32[]{:S(2)}) %all-to-all-start.1) | async-done | bytes 16777248 | tf_op jit(solution)/shard_map/all_to_all | solution.py:77
  310.0 15.6 %fusion = bf16[64,128,256]{2,0,1:T(8,128)(2,1)S(1)} fusion(bf16[256,128,256]{2,1,0:T(8,128)(2,1)} %all-to-all-done.1, s32[256]{0:T(256)S(1)} %get-tuple-element.5), kind=kOutput, calls=%fused_computation | convolution fusion | flops 1073758208 | bytes 20972544 | tf_op jit(solution)/shard_map/gs,sqb->gqb/dot_general | solution.py:139
  325.6 4.6 %copy.67.exchange_ref = bf16[64,128,256]{2,1,0:T(8,128)(2,1)} copy(bf16[64,128,256]{2,0,1:T(8,128)(2,1)S(1)} %fusion) | data formatting | bytes 8388608 | tf_op jit(solution)/shard_map/gs,sqb->gqb/dot_general | solution.py:139
  330.2 10.7 %shard_map.82 = bf16[64,256,256]{2,1,0:T(8,128)(2,1)} custom-call(f32[64,512]{1,0:T(8,128)} %fusion.10.weight_ref, bf16[64,128,256]{2,1,0:T(8,128)(2,1)} %copy.67.exchange_ref, f32[256,512]{1,0:T(8,128)} %convert_bitcast_fusion.basis_t_ref, bf16[512,256]{1,0:T(8,128)(2,1)} %basis_ref.1, bf16[256,128]{1,0:T(8,128)(2,1)} %slice_bitcast_fusion.inner_t_ref), custom_call_target="tpu_custom_call" | custom-call | tf_op jit(solution)/shard_map/pallas_call | solution.py:37
  340.9 0.0 copy-done.1
  (7 shorter events, 0.1 us)
Async XLA Ops:
  0.0 2.6 copy-start
  10.5 46.4 %all-to-all-start = ((f32[128,2,640]{2,1,0:T(2,128)}), f32[128,2,640]{2,1,0:T(2,128)S(1)}, u32[]{:S(2)}, u32[]{:S(2)}) async-start(f32[128,2,640]{2,1,0:T(2,128)} %concatenate.7), calls=%async_computation | async-start | bytes 1310720 | tf_op jit(solution)/shard_map/all_to_all | solution.py:113
  56.9 10.2 %copy-start.3 = (bf16[4,512]{1,0:T(4,128)(2,1)S(1)}, bf16[4,512]{1,0:T(4,128)(2,1)}, u32[]{:S(2)}) copy-start(bf16[4,512]{1,0:T(4,128)(2,1)} %param.10) | copy-start | bytes 12292
  56.9 235.8 %copy-start.2 = (bf16[512,256]{1,0:T(8,128)(2,1)S(1)}, bf16[512,256]{1,0:T(8,128)(2,1)}, u32[]{:S(2)}) copy-start(bf16[512,256]{1,0:T(8,128)(2,1)} %basis_ref.1) | copy-start | bytes 786436
  56.9 253.1 %all-to-all-start.1 = ((bf16[256,128,256]{2,1,0:T(8,128)(2,1)}), bf16[256,128,256]{2,1,0:T(8,128)(2,1)}, u32[]{:S(2)}, u32[]{:S(2)}) async-start(bf16[256,128,256]{2,1,0:T(8,128)(2,1)} %copy.47), calls=%async_computation.1 | async-start | bytes 33554432 | tf_op jit(solution)/shard_map/all_to_all | solution.py:77
  295.5 45.5 %copy-start.1 = (f32[8,512]{1,0:T(8,128)S(1)}, f32[8,512]{1,0:T(8,128)}, u32[]{:S(2)}) copy-start(f32[8,512]{1,0:T(8,128)} %param.9) | copy-start | bytes 49156
